TPU v7x, 128 devices: a whole 4x4x4 slice. The times are simulated.
128 devices in a mesh: sec: 2 (over x_hi), head: 4 (over x_lo, core), ctx: 16 (over z, y).
Axes of the slice: x: 4 (x_hi: 2, x_lo: 2; x = x_hi * 2 + x_lo), y: 4, z: 4, core: 2. Of those that a mesh axis runs over, the one named last changes fastest.
Arguments:
- proposal_rows: bfloat16 [512, 8192], P('sec', 'ctx'), may hold values from -400 to 400
- norm_gain: bfloat16 [8192], P('ctx'), may hold values from 0.25 to 1.75
- query_weight: bfloat16 [8192, 8192], P('ctx', ('sec', 'head')), may hold values from -0.0625 to 0.0625
- key_weight: bfloat16 [8192, 8, 128], P('ctx', ('sec', 'head')), may hold values from -0.25 to 0.25
- value_weight: bfloat16 [8192, 8, 128], P('ctx', ('sec', 'head')), may hold values from -0.0625 to 0.0625
- out_weight: bfloat16 [8192, 8192], P(('sec', 'head'), 'ctx'), may hold values from -0.0625 to 0.0625
- context_keys: bfloat16 [32768, 8, 128], P('ctx', ('sec', 'head')), may hold values from -256 to 256
- context_values: bfloat16 [32768, 8, 128], P('ctx', ('sec', 'head')), may hold values from -5 to 5
- prefix_lengths: int32 [32], replicated, may hold values from 2048 to 32768, as said below
- parents: int32 [512], replicated, may hold values from -1 to 510, as said below
Outputs:
- block_output: bfloat16 [512, 8192], P(('sec', 'head'), 'ctx')
Inputs may be any that keep to these rules, and one draw needn't show every extreme that they name: `parents`: token i = 16 p + s of particle p has parent -1 when s = 0, else 16 q + s - 1 for some particle q <= p. `prefix_lengths`: some particle sees the whole context.
All inputs are finite; a program needn't handle non-finite values.
Results may differ from a plain program's by a relative error of at most 0.015.
The roundings to bfloat16 on the way count: a program that leaves them out, or rounds other values in their place, can miss the bound.
Values may be sent and summed in bfloat16 or wider, within the bound.
No kernel may reach another device: no remote copies, remote signals or barrier semaphores. Data moves between devices by JAX's collectives and lax.ppermute only.
A program may use at most 192 MiB of HBM per device.

v0:
```python
import math

import jax
import jax.numpy as jnp
from jax import lax
from jax.sharding import PartitionSpec as P

D = 8192
PROPOSALS = 16


NEGATIVE = -1e30
EPSILON = 1e-05


def merged(value, axis, join):
    pieces = jax.tree.map(lambda part: lax.all_gather(part, axis), value)
    head = jax.tree.map(lambda part: part[0], pieces)
    tail = jax.tree.map(lambda part: part[1:], pieces)
    subtotal, _ = lax.scan(lambda subtotal, share: (join(subtotal, share), None), head, tail)
    return subtotal


def ancestry(parents, query_rows, key_offset, key_amount):
    key_index = key_offset + jnp.arange(key_amount, dtype=jnp.int32)

    def advance(turn_index, carried):
        current, reached = carried
        reached = jnp.logical_or(reached, current[:, None] == key_index[None, :])
        upward = jnp.take(parents, jnp.maximum(current, 0))
        return (jnp.where(current >= 0, upward, -1), reached)

    initial = (query_rows, jnp.zeros((query_rows.shape[0], key_amount), dtype=bool))
    return lax.fori_loop(0, PROPOSALS, advance, initial)[1]


def absorb(carried, scores, visible, values):
    summed, highest, weight_sum = carried
    newest = jnp.maximum(highest, jnp.max(jnp.where(visible, scores, NEGATIVE), axis=2))
    weights = jnp.where(visible, jnp.exp(scores - newest[:, :, None]), 0.0)
    shrink = jnp.exp(highest - newest)
    weight_sum = weight_sum * shrink + jnp.sum(weights, axis=2)
    summed = summed * shrink[:, :, None] + jnp.einsum(
        "rgt,td->rgd", weights.astype(jnp.bfloat16), values, preferred_element_type=jnp.float32
    )
    return (summed, newest, weight_sum)


def empty_state(amount, groups, head_size):
    return (
        jnp.zeros((amount, groups, head_size), jnp.float32),
        jnp.full((amount, groups), NEGATIVE, jnp.float32),
        jnp.zeros((amount, groups), jnp.float32),
    )


def attend_rows(queries, query_rows, carried, context, tree_part, lengths_rows, parents):
    context_rows, context_vals, context_offset = context
    tree_rows, tree_vals, tree_offset = tree_part
    amount = queries.shape[0]
    head_size = context_rows.shape[1]
    grouped = queries.reshape(amount, -1, head_size)
    factor = 1.0 / math.sqrt(head_size)
    positions = context_offset + jnp.arange(context_rows.shape[0], dtype=jnp.int32)
    scores = (
        jnp.einsum("rgd,td->rgt", grouped, context_rows, preferred_element_type=jnp.float32)
        * factor
    )
    visible = (positions[None, :] < lengths_rows[:, None])[:, None, :]
    carried = absorb(carried, scores, visible, context_vals)
    tree_scores = (
        jnp.einsum("rgd,td->rgt", grouped, tree_rows, preferred_element_type=jnp.float32) * factor
    )
    tree_visible = ancestry(parents, query_rows, tree_offset, tree_rows.shape[0])[:, None, :]
    return absorb(carried, tree_scores, tree_visible, tree_vals)


def combine(earlier, later):
    summed_a, highest_a, weight_a = earlier
    summed_b, highest_b, weight_b = later
    highest = jnp.maximum(highest_a, highest_b)
    factor_a = jnp.exp(highest_a - highest)
    factor_b = jnp.exp(highest_b - highest)
    amount, groups = highest_a.shape
    joined = (
        summed_a.reshape(amount, groups, -1) * factor_a[:, :, None]
        + summed_b.reshape(amount, groups, -1) * factor_b[:, :, None]
    )
    return (joined.reshape(amount, -1), highest, weight_a * factor_a + weight_b * factor_b)


def settle(projected, squares, query_width, head_size):
    inverse = lax.rsqrt(squares / D + EPSILON)[:, None]
    scaled = projected * inverse
    queries = scaled[:, :query_width].astype(jnp.bfloat16)
    tree_rows = scaled[:, query_width : query_width + head_size].astype(jnp.bfloat16)
    tree_vals = scaled[:, query_width + head_size :].astype(jnp.bfloat16)
    return (queries, tree_rows, tree_vals)


def body(
    proposal_rows,
    norm_gain,
    query_weight,
    key_weight,
    value_weight,
    out_weight,
    context_keys,
    context_values,
    prefix_lengths,
    parents,
):
    gathered = lax.all_gather(proposal_rows, "sec", axis=0, tiled=True)
    gathered_wide = gathered.astype(jnp.float32)
    squares = jnp.sum(gathered_wide * gathered_wide, axis=1)
    scaled = (gathered_wide * norm_gain.astype(jnp.float32)[None, :]).astype(jnp.bfloat16)
    joined = jnp.concatenate([query_weight, key_weight[:, 0, :], value_weight[:, 0, :]], axis=1)
    partial_value = jnp.dot(scaled, joined, preferred_element_type=jnp.float32)
    query_width = query_weight.shape[1]
    head_size = key_weight.shape[2]
    groups = query_width // head_size
    total_rows = gathered.shape[0]
    turn_count = lax.axis_size("ctx")
    row_share = total_rows // turn_count
    position = lax.axis_index("ctx")
    context = (context_keys[:, 0, :], context_values[:, 0, :], position * context_keys.shape[0])
    lengths_rows = jnp.repeat(prefix_lengths, PROPOSALS)
    projected, summed_squares = lax.psum((partial_value, squares), "ctx")
    queries, tree_rows, tree_vals = settle(projected, summed_squares, query_width, head_size)
    tree_part = (
        lax.dynamic_slice_in_dim(tree_rows, position * row_share, row_share, 0),
        lax.dynamic_slice_in_dim(tree_vals, position * row_share, row_share, 0),
        position * row_share,
    )
    query_block = min(256, total_rows)
    block_count = total_rows // query_block

    def run_block(pieces):
        block_queries, block_lengths, block_rows = pieces
        return attend_rows(
            block_queries,
            block_rows,
            empty_state(query_block, groups, head_size),
            context,
            tree_part,
            block_lengths,
            parents,
        )

    summed, highest, weight_sum = lax.map(
        run_block,
        (
            queries.reshape(block_count, query_block, query_width),
            lengths_rows.reshape(block_count, query_block),
            jnp.arange(total_rows, dtype=jnp.int32).reshape(block_count, query_block),
        ),
    )
    summed, highest, weight_sum = merged(
        (
            summed.reshape(total_rows, query_width),
            highest.reshape(total_rows, groups),
            weight_sum.reshape(total_rows, groups),
        ),
        "ctx",
        combine,
    )
    attended = (
        (summed.reshape(total_rows, groups, head_size) / weight_sum[:, :, None])
        .reshape(total_rows, query_width)
        .astype(jnp.bfloat16)
    )
    return lax.psum_scatter(
        jnp.dot(attended, out_weight, preferred_element_type=jnp.float32).astype(jnp.bfloat16),
        ("sec", "head"),
        scatter_dimension=0,
        tiled=True,
    )


def solution(mesh):
    placed = (
        P("sec", "ctx"),
        P("ctx"),
        P("ctx", ("sec", "head")),
        P("ctx", ("sec", "head"), None),
        P("ctx", ("sec", "head"), None),
        P(("sec", "head"), "ctx"),
        P("ctx", ("sec", "head"), None),
        P("ctx", ("sec", "head"), None),
        P(),
        P(),
    )
    return jax.shard_map(
        body, mesh=mesh, in_specs=placed, out_specs=P(("sec", "head"), "ctx"), check_vma=False
    )
```

profile of v0, /device:TPU:1, one launch (start us, length us, event | category | flops | bytes accessed | tf_op | source)
XLA Modules:
  0.0 616.0 jit_solution(15716982886982336540)
XLA Ops:
  6.5 10.3 %all_gather.12 = bf16[512,512]{1,0:T(8,128)(2,1)S(1)} all-gather(bf16[256,512]{1,0:T(8,128)(2,1)} %param.16), channel_id=1, replica_groups=mesh['sec'=2,'head'=4,'ctx'=16] {'sec'}, dimensions={0}, use_global_device_ids=true | all-gather | bytes 786432 | tf_op jit(solution)/shard_map/all_gather | solution.py:113
  17.5 3.7 fusion.39
  22.3 35.2 %psum.15 = f32[512]{0:T(512)S(1)} all-reduce(f32[512]{0:T(512)S(1)} %fusion.46), channel_id=1, replica_groups=mesh['sec'=2,'head'=4,'ctx'=16] {'ctx'}, use_global_device_ids=true, to_apply=%region_2.0 | all-reduce | flops 512 | bytes 4096 | tf_op jit(solution)/shard_map/psum | solution.py:128
  57.5 60.0 %all-reduce.2.cloned.1.call-done = f32[512,1280]{1,0:T(8,128)} async-done(((f32[512,1280]{1,0:T(8,128)}), f32[512,1280]{1,0:T(8,128)}) %all-reduce.2.cloned.1.call-update) | async-done | bytes 2621456 | tf_op jit(solution)/shard_map/psum | solution.py:128
  120.6 104.0 %while.42 = (s32[]{:T(128)}, f32[2,256,8,128]{3,2,1,0:T(8,128)}, f32[2,256,8]{1,2,0:T(8,128)S(1)}, f32[2,256,8]{1,2,0:T(8,128)S(1)}, s32[]{:T(128)}, /*index=5*/...) while((s32[]{:T(128)}, f32[2,256,8,128]{3,2,1,0:T(8,128)}, ...), condition=%wide.region_10.11_spmd, body=%wide.region_3.10_spmd.sunk | while | flops 2229123584 | bytes 62943320 | solution.py:150
  120.6 34.7 %while.44 = (s32[]{:T(128)}, s32[256]{0:T(256)S(1)}, pred[256,32]{1,0:T(8,128)(4,1)S(1)}, s32[512]{0:T(512)S(1)}, s32[]{:T(128)}, /*index=5*/s32[]{:T(128)}, s32[]{:T(128)}) while((s32[]{:T(128)}, s32[256]{0:T(256)S(1)}, pred[256,32]{1,0:T(8,128)(4,1)S(1)}, s32[512]{0:T(512)S(1)}, s32[]{:T(128)}, /*index=5*/s32[]{:T(128)}, ...), condition=%wide.region_6.6_spmd.clone, body=%wide.region_5.5_spmd.clone.sunk | while | flops 27171 | bytes 31067 | solution.py:34
  157.3 3.6 select_reduce_fusion.4
  160.9 4.6 fusion.80
  165.6 5.0 fusion.77
  172.6 34.7 %while.44 = (s32[]{:T(128)}, s32[256]{0:T(256)S(1)}, pred[256,32]{1,0:T(8,128)(4,1)S(1)}, s32[512]{0:T(512)S(1)}, s32[]{:T(128)}, /*index=5*/s32[]{:T(128)}, s32[]{:T(128)}) while((s32[]{:T(128)}, s32[256]{0:T(256)S(1)}, pred[256,32]{1,0:T(8,128)(4,1)S(1)}, s32[512]{0:T(512)S(1)}, s32[]{:T(128)}, /*index=5*/s32[]{:T(128)}, ...), condition=%wide.region_6.6_spmd.clone, body=%wide.region_5.5_spmd.clone.sunk | while | flops 27171 | bytes 31067 | solution.py:34
  209.2 3.6 select_reduce_fusion.4
  212.8 4.6 fusion.80
  217.5 5.0 fusion.77
  224.5 2.7 all_gather_reshape.9
  227.3 17.5 %all_gather.14 = f32[16,512,8]{1,2,0:T(8,128)S(1)} all-gather(f32[1,512,8]{1,2,0:T(8,128)S(1)} %bitcast.151), channel_id=1, replica_groups=mesh['sec'=2,'head'=4,'ctx'=16] {'ctx'}, dimensions={0}, use_global_device_ids=true | all-gather | bytes 278528 | tf_op jit(solution)/shard_map/all_gather | solution.py:17
  245.7 20.9 %all_gather.15 = f32[16,512,8]{1,2,0:T(8,128)S(1)} all-gather(f32[1,512,8]{1,2,0:T(8,128)S(1)} %bitcast.152), channel_id=1, replica_groups=mesh['sec'=2,'head'=4,'ctx'=16] {'ctx'}, dimensions={0}, use_global_device_ids=true | all-gather | bytes 278528 | tf_op jit(solution)/shard_map/all_gather | solution.py:17
  268.2 157.7 %all-gather.2.cloned.1.call-done = f32[16,512,1024]{2,1,0:T(8,128)} async-done(((f32[1,512,1024]{2,1,0:T(8,128)}), f32[16,512,1024]{2,1,0:T(8,128)}) %all-gather.2.cloned.1.call-update) | async-done | bytes 33554448 | tf_op jit(solution)/shard_map/all_gather | solution.py:17
  425.9 22.4 %slice.48 = f32[15,512,1024]{2,1,0:T(8,128)} slice(f32[16,512,1024]{2,1,0:T(8,128)} %all-gather.2.cloned.1.call-done), slice={[1:16], [0:512], [0:1024]} | slice | bytes 62914560 | tf_op jit(solution)/shard_map/slice | solution.py:19
  450.1 127.7 %while.43 = (s32[]{:T(128)}, f32[512,1024]{1,0:T(8,128)S(1)}, f32[512,8]{1,0:T(8,128)}, f32[512,8]{1,0:T(8,128)}, f32[15,512,8]{1,2,0:T(8,128)S(1)}, /*index=5*/...) while((s32[]{:T(128)}, f32[512,1024]{1,0:T(8,128)S(1)}, f32[512,8]{1,0:T(8,128)}, ...), condition=%wide.region_12.13_spmd, body=%wide.region_11.12_spmd.sunk | while | flops 1597442 | bytes 16941204 | solution.py:20
  451.8 2.0 fusion.82
  455.1 3.5 fusion.83
  460.4 2.0 fusion.82
  463.6 3.5 fusion.83
  468.9 2.0 fusion.82
  472.1 3.5 fusion.83
  477.4 2.0 fusion.82
  480.6 3.5 fusion.83
  485.9 2.0 fusion.82
  489.1 3.5 fusion.83
  494.4 2.0 fusion.82
  497.6 3.5 fusion.83
  502.9 2.0 fusion.82
  506.1 3.5 fusion.83
  511.4 2.0 fusion.82
  514.7 3.5 fusion.83
  519.9 2.0 fusion.82
  523.2 3.5 fusion.83
  528.4 2.0 fusion.82
  531.7 3.5 fusion.83
  537.0 2.0 fusion.82
  540.2 3.5 fusion.83
  545.5 2.0 fusion.82
  548.7 3.5 fusion.83
  554.0 2.0 fusion.82
  557.2 3.5 fusion.83
  565.7 3.5 fusion.83
  574.2 3.5 fusion.83
  580.9 28.6 %reduce-scatter.2.cloned.1.call-done = bf16[64,512]{1,0:T(8,128)(2,1)} async-done(((bf16[512,512]{1,0:T(8,128)(2,1)}), bf16[64,512]{1,0:T(8,128)(2,1)}) %reduce-scatter.2.cloned.1.call-update) | async-done | bytes 65552 | tf_op jit(solution)/shard_map/reduce_scatter | solution.py:172
  (394 shorter events, 135.9 us)
Async XLA Ops:
  6.5 572.8 %copy-start = (bf16[1024,512]{1,0:T(8,128)(2,1)S(1)}, bf16[1024,512]{1,0:T(8,128)(2,1)}, u32[]{:S(2)}) copy-start(bf16[1024,512]{1,0:T(8,128)(2,1)} %param.21) | copy-start | bytes 3145732
  6.5 110.9 %all-reduce.2.cloned.1.call-start = ((), (), s32[]{:S(2)}) async-start(), calls=%async_computation.1 | async-start | bytes 5242880 | tf_op jit(solution)/shard_map/psum | solution.py:128
  21.2 0.7 copy-start.6
  21.3 404.7 %all-gather.2.cloned.1.call-start = ((), (), s32[]{:S(2)}) async-start(), calls=%async_computation.2 | async-start | bytes 35651584 | tf_op jit(solution)/shard_map/all_gather | solution.py:17
  57.5 63.1 %copy-start.1 = (s32[512]{0:T(512)S(1)}, s32[512]{0:T(512)}, u32[]{:S(2)}) copy-start(s32[512]{0:T(512)} %param.25) | copy-start | bytes 6148
  57.5 63.1 %copy-start.2 = (bf16[2048,1,128]{2,0,1:T(8,128)(2,1)S(1)}, bf16[2048,1,128]{2,0,1:T(8,128)(2,1)}, u32[]{:S(2)}) copy-start(bf16[2048,1,128]{2,0,1:T(8,128)(2,1)} %param.22) | copy-start | bytes 1572868
  57.5 63.1 %copy-start.5 = (bf16[2048,1,128]{2,0,1:T(8,128)(2,1)S(1)}, bf16[2048,1,128]{2,0,1:T(8,128)(2,1)}, u32[]{:S(2)}) copy-start(bf16[2048,1,128]{2,0,1:T(8,128)(2,1)} %param.23) | copy-start | bytes 1572868
  227.3 382.2 %reduce-scatter.2.cloned.1.call-start = ((), (), s32[]{:S(2)}) async-start(), calls=%async_computation.3 | async-start | bytes 589824 | tf_op jit(solution)/shard_map/reduce_scatter | solution.py:172
  450.1 0.8 copy-start.3
  455.1 3.5 copy-start.4
  458.6 0.8 copy-start.3
  463.6 3.5 copy-start.4
  467.1 0.8 copy-start.3
  472.1 3.5 copy-start.4
  475.6 0.8 copy-start.3
  480.6 3.5 copy-start.4
  484.1 0.8 copy-start.3
  489.1 3.5 copy-start.4
  492.7 0.8 copy-start.3
  497.6 3.5 copy-start.4
  501.2 0.8 copy-start.3
  506.1 3.5 copy-start.4
  509.7 0.8 copy-start.3
  514.6 3.5 copy-start.4
  518.2 0.8 copy-start.3
  523.2 3.5 copy-start.4
  526.7 0.8 copy-start.3
  531.7 3.5 copy-start.4
  535.2 0.8 copy-start.3
  540.2 3.5 copy-start.4
  543.7 0.8 copy-start.3
  548.7 3.5 copy-start.4
  552.2 0.8 copy-start.3
  557.2 3.5 copy-start.4
  560.7 0.8 copy-start.3
  565.7 3.5 copy-start.4
  569.3 0.8 copy-start.3
  574.2 3.5 copy-start.4
Sparse Core Ops, SparseCore 0:
  21.4 96.0 all-reduce.1
  227.4 198.5 all-gather.1
  581.0 28.4 reduce-scatter.1
where the time goes:
time: 620 us; the launch traced here: 616 us
  waiting for transfers between devices  246 us (40%)
  local copies, waits for them, and re-layouts  145 us (23%)
  other arithmetic  101 us (16%)
  blocking collectives  83.9 us (14%)
  matrix products  23.5 us (4%)
  between operations  13.2 us (2%)
    all_gather x1, waiting for transfers between devices, merged(): pieces = jax.tree.map(lambda part: lax.all_gather(part, axis), value)  158 us
    gather x32, local copies, waits for them, and re-layouts, advance(): upward = jnp.take(parents, jnp.maximum(current, 0))  62.2 us
    psum x1, waiting for transfers between devices, body(): projected, summed_squares = lax.psum((partial_value, squares), 'ctx')  60 us
    add x15, other arithmetic, combine(): summed_a.reshape(amount, groups, -1) * factor_a[:, :, None]  52.6 us
    all_gather x2, blocking collectives, merged(): pieces = jax.tree.map(lambda part: lax.all_gather(part, axis), value)  38.4 us
    psum x1, blocking collectives, body(): projected, summed_squares = lax.psum((partial_value, squares), 'ctx')  35.2 us
    add x15, other arithmetic, combine(): weight_a * factor_a + weight_b * factor_b  30.2 us
    reduce_scatter x1, waiting for transfers between devices, body(): lax.psum_scatter(jnp.dot(attended, out_weight, preferred_element_type=jnp...  28.6 us
  transfers between devices with their start and end apart: 3, of which 3 were waited for; matrix products, arithmetic and copies ran while one was open for 0% of the time, Pallas kernels for 0%

commit v1 on v0

v1 whole, which is shorter than its diff:
```python
import math

import jax
import jax.numpy as jnp
from jax import lax
from jax.sharding import PartitionSpec as P

D = 8192
PROPOSALS = 16


NEGATIVE = -1e30
EPSILON = 1e-05


def ancestry_columns(parents, column_offset, column_amount):
    total = parents.shape[0]
    index = jnp.arange(total, dtype=jnp.int32)
    step = jnp.logical_or(parents[:, None] == index[None, :], index[:, None] == index[None, :])
    reach = step.astype(jnp.bfloat16)
    for _ in range(3):
        reach = (jnp.dot(reach, reach, preferred_element_type=jnp.float32) > 0).astype(jnp.bfloat16)
    columns = lax.dynamic_slice_in_dim(reach, column_offset, column_amount, 1)
    return jnp.dot(reach, columns, preferred_element_type=jnp.float32) > 0


def body(
    proposal_rows,
    norm_gain,
    query_weight,
    key_weight,
    value_weight,
    out_weight,
    context_keys,
    context_values,
    prefix_lengths,
    parents,
):
    gathered = lax.all_gather(proposal_rows, "sec", axis=0, tiled=True)
    gathered_wide = gathered.astype(jnp.float32)
    total_rows = gathered.shape[0]
    squares = jnp.sum(gathered_wide * gathered_wide, axis=1)
    scaled = (gathered_wide * norm_gain.astype(jnp.float32)[None, :]).astype(jnp.bfloat16)
    query_width = query_weight.shape[1]
    head_size = key_weight.shape[2]
    groups = query_width // head_size
    joined = jnp.concatenate([query_weight, key_weight[:, 0, :], value_weight[:, 0, :]], axis=1)
    partial_value = jnp.dot(scaled, joined, preferred_element_type=jnp.float32)
    proj_width = partial_value.shape[1]
    lane = jnp.arange(128, dtype=jnp.int32)
    square_block = jnp.where(lane[None, :] == 0, squares[:, None], 0.0)
    packed = jnp.concatenate([partial_value, square_block], axis=1)
    reduced = lax.psum_scatter(packed, "ctx", scatter_dimension=0, tiled=True)
    row_share = reduced.shape[0]
    inverse = lax.rsqrt(reduced[:, proj_width] / D + EPSILON)[:, None]
    settled = reduced[:, :proj_width] * inverse
    own_queries = settled[:, :query_width].astype(jnp.bfloat16)
    tree_keys = settled[:, query_width : query_width + head_size].astype(jnp.bfloat16)
    tree_vals = settled[:, query_width + head_size :].astype(jnp.bfloat16)
    queries = lax.all_gather(own_queries, "ctx", axis=0, tiled=True)

    position = lax.axis_index("ctx")
    keys = context_keys[:, 0, :]
    vals = context_values[:, 0, :]
    span = keys.shape[0]
    factor = 1.0 / math.sqrt(head_size)
    grouped = queries.reshape(total_rows, groups, head_size)
    lengths_rows = jnp.repeat(prefix_lengths, PROPOSALS)
    positions = position * span + jnp.arange(span, dtype=jnp.int32)
    visible = (positions[None, :] < lengths_rows[:, None])[:, None, :]
    scores = jnp.einsum("rgd,td->rgt", grouped, keys, preferred_element_type=jnp.float32) * factor
    tree_visible = ancestry_columns(parents, position * row_share, row_share)[:, None, :]
    tree_scores = (
        jnp.einsum("rgd,td->rgt", grouped, tree_keys, preferred_element_type=jnp.float32) * factor
    )
    local_high = jnp.maximum(
        jnp.max(jnp.where(visible, scores, NEGATIVE), axis=2),
        jnp.max(jnp.where(tree_visible, tree_scores, NEGATIVE), axis=2),
    )
    highest = lax.pmax(local_high, "ctx")
    weights = jnp.where(visible, jnp.exp(scores - highest[:, :, None]), 0.0)
    tree_weights = jnp.where(tree_visible, jnp.exp(tree_scores - highest[:, :, None]), 0.0)
    weight_sum = jnp.sum(weights, axis=2) + jnp.sum(tree_weights, axis=2)
    summed = jnp.einsum(
        "rgt,td->rgd", weights.astype(jnp.bfloat16), vals, preferred_element_type=jnp.float32
    ) + jnp.einsum(
        "rgt,td->rgd", tree_weights.astype(jnp.bfloat16), tree_vals, preferred_element_type=jnp.float32
    )
    sum_block = jnp.concatenate(
        [weight_sum, jnp.zeros((total_rows, 128 - groups), jnp.float32)], axis=1
    )
    packed_attn = jnp.concatenate([summed.reshape(total_rows, query_width), sum_block], axis=1)
    merged = lax.psum_scatter(packed_attn, "ctx", scatter_dimension=0, tiled=True)
    own_attended = (
        (merged[:, :query_width].reshape(row_share, groups, head_size)
         / merged[:, query_width : query_width + groups][:, :, None])
        .reshape(row_share, query_width)
        .astype(jnp.bfloat16)
    )
    attended = lax.all_gather(own_attended, "ctx", axis=0, tiled=True)
    return lax.psum_scatter(
        jnp.dot(attended, out_weight, preferred_element_type=jnp.float32).astype(jnp.bfloat16),
        ("sec", "head"),
        scatter_dimension=0,
        tiled=True,
    )


def solution(mesh):
    placed = (
        P("sec", "ctx"),
        P("ctx"),
        P("ctx", ("sec", "head")),
        P("ctx", ("sec", "head"), None),
        P("ctx", ("sec", "head"), None),
        P(("sec", "head"), "ctx"),
        P("ctx", ("sec", "head"), None),
        P("ctx", ("sec", "head"), None),
        P(),
        P(),
    )
    return jax.shard_map(
        body, mesh=mesh, in_specs=placed, out_specs=P(("sec", "head"), "ctx"), check_vma=False
    )
```

time: 620 us -> 427 us (0.69)
  local copies, waits for them, and re-layouts: 145 us -> 5.52 us
  other arithmetic: 101 us -> 20.8 us
  waiting for transfers between devices: 246 us -> 275 us
  matrix products: 23.5 us -> 41.4 us
  blocking collectives: 83.9 us -> 68.1 us
    unnamed x3 -> x6, waiting for transfers between devices: 0.05 us -> 86.6 us
    add x64 -> x2, other arithmetic: 83 us -> 0.01 us  [the longest x1 0.01 us: body(): weight_sum = jnp.sum(weights, axis=2) + jnp.sum(tree_weights, axis=2)]
    reduce_scatter x0 -> x1, waiting for transfers between devices: none -> 78.4 us  [body(): reduced = lax.psum_scatter(packed, 'ctx', scatter_dimension=0, tiled=True)]
    all_gather x1 -> x2, waiting for transfers between devices: 158 us -> 80.5 us  [the longest x1 41.8 us: body(): attended = lax.all_gather(own_attended, 'ctx', axis=0, tiled=True)]
    gather x32 -> x0, local copies, waits for them, and re-layouts: 62.2 us -> none  [advance(): upward = jnp.take(parents, jnp.maximum(current, 0))]
    psum x1 -> x0, waiting for transfers between devices: 60 us -> none  [body(): projected, summed_squares = lax.psum((partial_value, squares), 'ctx')]
    pmax x0 -> x1, blocking collectives: none -> 57.8 us  [body(): highest = lax.pmax(local_high, 'ctx')]
    all_gather x2 -> x0, blocking collectives: 38.4 us -> none  [merged(): pieces = jax.tree.map(lambda part: lax.all_gather(part, axis), value)]
  transfers between devices with their start and end apart: 3 -> 5, of which waited for: 3 -> 5; matrix products, arithmetic and copies ran while one was open for 0% -> 1% of each run, Pallas kernels for 0% -> 0%
where the time goes in v1:
time: 427 us; the launch traced here: 425 us
  waiting for transfers between devices  275 us (64%)
  blocking collectives  68.1 us (16%)
  matrix products  41.4 us (10%)
  other arithmetic  20.8 us (5%)
  between operations  13.3 us (3%)
  local copies, waits for them, and re-layouts  5.52 us (1%)
    unnamed x6, waiting for transfers between devices  86.6 us
    reduce_scatter x1, waiting for transfers between devices, body(): reduced = lax.psum_scatter(packed, 'ctx', scatter_dimension=0, tiled=True)  78.4 us
    pmax x1, blocking collectives, body(): highest = lax.pmax(local_high, 'ctx')  57.8 us
    all_gather x1, waiting for transfers between devices, body(): attended = lax.all_gather(own_attended, 'ctx', axis=0, tiled=True)  41.8 us
    all_gather x1, waiting for transfers between devices, body(): queries = lax.all_gather(own_queries, 'ctx', axis=0, tiled=True)  38.7 us
    reduce_scatter x1, waiting for transfers between devices, body(): lax.psum_scatter(jnp.dot(attended, out_weight, preferred_element_type=jnp...  29.9 us
    dot_general x1, matrix products, body(): jnp.einsum('rgt,td->rgd', weights.astype(jnp.bfloat16), vals, preferred_e...  15.4 us
    reduce_sum x2, other arithmetic, body(): weight_sum = jnp.sum(weights, axis=2) + jnp.sum(tree_weights, axis=2)  15.3 us
  transfers between devices with their start and end apart: 5, of which 5 were waited for; matrix products, arithmetic and copies ran while one was open for 1% of the time, Pallas kernels for 0%

profile of v1, /device:TPU:1, one launch (start us, length us, event | category | flops | bytes accessed | tf_op | source)
XLA Modules:
  0.0 424.7 jit_solution(10706751456148544928)
XLA Ops:
  6.5 0.0 copy-start
  6.5 10.3 %all_gather.9 = bf16[512,512]{1,0:T(8,128)(2,1)S(1)} all-gather(bf16[256,512]{1,0:T(8,128)(2,1)} %param.10), channel_id=1, replica_groups=mesh['sec'=2,'head'=4,'ctx'=16] {'sec'}, dimensions={0}, use_global_device_ids=true | all-gather | bytes 786432 | tf_op jit(solution)/shard_map/all_gather | solution.py:39
  16.8 0.7 convert_element_type.29
  17.5 0.2 fusion.12
  17.7 0.1 broadcast_select_fusion
  17.8 2.2 fusion.5
  20.1 1.8 pad_maximum_fusion
  21.8 0.0 reduce-scatter.6.cloned.1.call-update
  21.9 0.0 all-gather.3.cloned.1.call-start
  21.9 78.4 %reduce-scatter.6.cloned.1.call-done = f32[32,1408]{1,0:T(8,128)} async-done(((f32[512,1408]{1,0:T(8,128)}), f32[32,1408]{1,0:T(8,128)}) %reduce-scatter.6.cloned.1.call-update) | async-done | bytes 180240 | tf_op jit(solution)/shard_map/reduce_scatter | solution.py:53
  100.3 0.8 fusion.37
  101.1 1.0 fusion.34
  102.2 0.6 slice.33
  102.8 0.0 all-gather.3.cloned.1.call-update
  102.8 0.0 reduce-scatter.10.cloned.1.call-start
  102.9 0.1 broadcast_in_dim.76
  102.9 0.1 lt.23
  103.0 0.1 pad.2.clone
  103.1 0.6 convolution_compare_fusion.2
  103.8 0.0 copy-start.1
  103.8 1.1 convolution_compare_fusion
  104.9 0.4 convolution_compare_fusion.3
  105.3 0.7 broadcast_compare_fusion
  106.0 38.7 %all-gather.3.cloned.1.call-done = bf16[512,1024]{1,0:T(8,128)(2,1)} async-done(((bf16[32,1024]{1,0:T(8,128)(2,1)}), bf16[512,1024]{1,0:T(8,128)(2,1)}) %all-gather.3.cloned.1.call-update) | async-done | bytes 1048592 | tf_op jit(solution)/shard_map/all_gather | solution.py:60
  144.6 1.7 select_reduce_fusion.1
  146.4 15.1 %select_reduce_fusion = (f32[512,8]{0,1:T(8,128)S(1)}, f32[512,8,2048]{2,0,1:T(8,128)}) fusion(pred[512,2048]{1,0:T(8,128)(4,1)S(1)} %broadcast_compare_fusion, bf16[2048,1,128]{2,0,1:T(8,128)(2,1)S(1)} %copy-done.1, bf16[512,1024]{1,0:T(8,128)(2,1)} %all-gather.3.cloned.1.call-done), kind=kOutput, calls=%fused_computation.1 | convolution fusion | flops 2172645376 | bytes 36192256 | tf_op jit(solution)/shard_map/rgd,td->rgt/dot_general | solution.py:71
  161.5 57.8 %pmax.7 = f32[512,8]{0,1:T(8,128)S(1)} all-reduce(f32[512,8]{0,1:T(8,128)S(1)} %max.5), channel_id=1, replica_groups=mesh['sec'=2,'head'=4,'ctx'=16] {'ctx'}, use_global_device_ids=true, to_apply=%region_4.5 | all-reduce | flops 4096 | bytes 32768 | tf_op jit(solution)/shard_map/pmax | solution.py:80
  219.3 15.2 %fusion = f32[512,8]{0,1:T(8,128)S(1)} fusion(f32[512,8,2048]{2,0,1:T(8,128)} %get-tuple-element.6, f32[512,8]{0,1:T(8,128)S(1)} %pmax.7, pred[512,2048]{1,0:T(8,128)(4,1)S(1)} %broadcast_compare_fusion), kind=kLoop, calls=%fused_computation.2 | loop fusion | flops 33550336 | bytes 34635776 | tf_op jit(solution)/shard_map/reduce_sum | solution.py:83
  234.5 15.4 %fusion.2 = f32[512,8,128]{0,2,1:T(8,128)} fusion(f32[512,8,2048]{2,0,1:T(8,128)} %get-tuple-element.6, f32[512,8]{0,1:T(8,128)S(1)} %pmax.7, pred[512,2048]{1,0:T(8,128)(4,1)S(1)} %broadcast_compare_fusion, bf16[2048,1,128]{2,0,1:T(8,128)(2,1)} %param.17), kind=kOutput, calls=%fused_computation.4 | convolution fusion | flops 2181038080 | bytes 37240832 | tf_op jit(solution)/shard_map/rgt,td->rgd/dot_general | solution.py:84
  249.9 0.1 fusion.27
  250.0 2.1 convolution_add_fusion
  252.1 0.2 maximum_maximum_fusion
  252.3 2.0 copy.25
  254.3 0.0 reduce-scatter.10.cloned.1.call-update
  254.4 0.0 all-gather.5.cloned.1.call-start
  254.4 86.5 %reduce-scatter.10.cloned.1.call-done = f32[32,1152]{1,0:T(8,128)} async-done(((f32[512,1152]{1,0:T(8,128)}), f32[32,1152]{1,0:T(8,128)}) %reduce-scatter.10.cloned.1.call-update) | async-done | bytes 147472
  340.9 0.9 slice.36
  341.9 0.2 copy.27
  342.1 0.7 slice.37
  342.8 0.1 copy.28
  342.9 0.1 fusion.22
  342.9 0.8 copy.21
  343.7 0.0 all-gather.5.cloned.1.call-update
  343.7 0.0 reduce-scatter.8.cloned.1.call-start
  343.7 41.8 %all-gather.5.cloned.1.call-done = bf16[512,1024]{1,0:T(8,128)(2,1)} async-done(((bf16[32,1024]{1,0:T(8,128)(2,1)}), bf16[512,1024]{1,0:T(8,128)(2,1)}) %all-gather.5.cloned.1.call-update) | async-done | bytes 1048592 | tf_op jit(solution)/shard_map/all_gather | solution.py:100
  385.6 2.8 convolution_convert_fusion
  388.3 0.0 reduce-scatter.8.cloned.1.call-update
  388.3 29.9 %reduce-scatter.8.cloned.1.call-done = bf16[64,512]{1,0:T(8,128)(2,1)} async-done(((bf16[512,512]{1,0:T(8,128)(2,1)}), bf16[64,512]{1,0:T(8,128)(2,1)}) %reduce-scatter.8.cloned.1.call-update) | async-done | bytes 65552 | tf_op jit(solution)/shard_map/reduce_scatter | solution.py:101
  (12 shorter events, 0.0 us)
Async XLA Ops:
  6.5 379.0 %copy-start = (bf16[1024,512]{1,0:T(8,128)(2,1)S(1)}, bf16[1024,512]{1,0:T(8,128)(2,1)}, u32[]{:S(2)}) copy-start(bf16[1024,512]{1,0:T(8,128)(2,1)} %param.15) | copy-start | bytes 3145732
  6.5 93.8 %reduce-scatter.6.cloned.1.call-start = ((), (), s32[]{:S(2)}) async-start(), calls=%async_computation.3 | async-start | bytes 3063808 | tf_op jit(solution)/shard_map/reduce_scatter | solution.py:53
  21.8 81.0 %copy-start.2 = (s32[32]{0:T(128)S(1)}, s32[32]{0:T(128)}, u32[]{:S(2)}) copy-start(s32[32]{0:T(128)} %param.18) | copy-start | bytes 388
  21.8 81.3 %copy-start.3 = (s32[512]{0:T(512)S(1)}, s32[512]{0:T(512)}, u32[]{:S(2)}) copy-start(s32[512]{0:T(512)} %param.19) | copy-start | bytes 6148
  21.9 122.8 %all-gather.3.cloned.1.call-start = ((), (), s32[]{:S(2)}) async-start(), calls=%async_computation.4 | async-start | bytes 1114112 | tf_op jit(solution)/shard_map/all_gather | solution.py:60
  102.8 238.1 %reduce-scatter.10.cloned.1.call-start = ((), (), s32[]{:S(2)}) async-start(), calls=%async_computation.7 | async-start | bytes 2506752
  103.8 42.6 %copy-start.1 = (bf16[2048,1,128]{2,0,1:T(8,128)(2,1)S(1)}, bf16[2048,1,128]{2,0,1:T(8,128)(2,1)}, u32[]{:S(2)}) copy-start(bf16[2048,1,128]{2,0,1:T(8,128)(2,1)} %param.16) | copy-start | bytes 1572868
  254.4 131.2 %all-gather.5.cloned.1.call-start = ((), (), s32[]{:S(2)}) async-start(), calls=%async_computation.5 | async-start | bytes 1114112 | tf_op jit(solution)/shard_map/all_gather | solution.py:100
  343.7 74.5 %reduce-scatter.8.cloned.1.call-start = ((), (), s32[]{:S(2)}) async-start(), calls=%async_computation.6 | async-start | bytes 589824 | tf_op jit(solution)/shard_map/reduce_scatter | solution.py:101
Sparse Core Ops, SparseCore 0:
  22.0 78.2 reduce-scatter.5
  102.9 41.6 all-gather.2
  254.5 86.4 reduce-scatter.9
  343.8 41.6 all-gather.4
  388.4 29.6 reduce-scatter.7

commit v2 on v1

--- a/solution.py
+++ b/solution.py
@@ -24,6 +24,17 @@
     return jnp.dot(reach, columns, preferred_element_type=jnp.float32) > 0
 
 
+def reduce_rows(value, axis):
+    count = lax.axis_size(axis)
+    moved = lax.all_to_all(value, axis, 0, 0, tiled=True)
+    return jnp.sum(moved.reshape(count, -1, *value.shape[1:]), axis=0)
+
+
+def gather_rows(value, axis):
+    count = lax.axis_size(axis)
+    return lax.all_to_all(jnp.tile(value, (count, 1)), axis, 0, 0, tiled=True)
+
+
 def body(
     proposal_rows,
     norm_gain,
@@ -36,7 +47,13 @@
     prefix_lengths,
     parents,
 ):
-    gathered = lax.all_gather(proposal_rows, "sec", axis=0, tiled=True)
+    other_rows = lax.ppermute(proposal_rows, "sec", [(0, 1), (1, 0)])
+    first = lax.axis_index("sec") == 0
+    gathered = jnp.where(
+        first,
+        jnp.concatenate([proposal_rows, other_rows], axis=0),
+        jnp.concatenate([other_rows, proposal_rows], axis=0),
+    )
     gathered_wide = gathered.astype(jnp.float32)
     total_rows = gathered.shape[0]
     squares = jnp.sum(gathered_wide * gathered_wide, axis=1)
@@ -50,14 +67,14 @@
     lane = jnp.arange(128, dtype=jnp.int32)
     square_block = jnp.where(lane[None, :] == 0, squares[:, None], 0.0)
     packed = jnp.concatenate([partial_value, square_block], axis=1)
-    reduced = lax.psum_scatter(packed, "ctx", scatter_dimension=0, tiled=True)
+    reduced = reduce_rows(packed, "ctx")
     row_share = reduced.shape[0]
     inverse = lax.rsqrt(reduced[:, proj_width] / D + EPSILON)[:, None]
     settled = reduced[:, :proj_width] * inverse
     own_queries = settled[:, :query_width].astype(jnp.bfloat16)
     tree_keys = settled[:, query_width : query_width + head_size].astype(jnp.bfloat16)
     tree_vals = settled[:, query_width + head_size :].astype(jnp.bfloat16)
-    queries = lax.all_gather(own_queries, "ctx", axis=0, tiled=True)
+    queries = gather_rows(own_queries, "ctx")
 
     position = lax.axis_index("ctx")
     keys = context_keys[:, 0, :]
@@ -77,33 +94,33 @@
         jnp.max(jnp.where(visible, scores, NEGATIVE), axis=2),
         jnp.max(jnp.where(tree_visible, tree_scores, NEGATIVE), axis=2),
     )
-    highest = lax.pmax(local_high, "ctx")
-    weights = jnp.where(visible, jnp.exp(scores - highest[:, :, None]), 0.0)
-    tree_weights = jnp.where(tree_visible, jnp.exp(tree_scores - highest[:, :, None]), 0.0)
+    weights = jnp.where(visible, jnp.exp(scores - local_high[:, :, None]), 0.0)
+    tree_weights = jnp.where(tree_visible, jnp.exp(tree_scores - local_high[:, :, None]), 0.0)
     weight_sum = jnp.sum(weights, axis=2) + jnp.sum(tree_weights, axis=2)
     summed = jnp.einsum(
         "rgt,td->rgd", weights.astype(jnp.bfloat16), vals, preferred_element_type=jnp.float32
     ) + jnp.einsum(
         "rgt,td->rgd", tree_weights.astype(jnp.bfloat16), tree_vals, preferred_element_type=jnp.float32
     )
-    sum_block = jnp.concatenate(
-        [weight_sum, jnp.zeros((total_rows, 128 - groups), jnp.float32)], axis=1
+    side_block = jnp.concatenate(
+        [weight_sum, local_high, jnp.zeros((total_rows, 128 - 2 * groups), jnp.float32)], axis=1
     )
-    packed_attn = jnp.concatenate([summed.reshape(total_rows, query_width), sum_block], axis=1)
-    merged = lax.psum_scatter(packed_attn, "ctx", scatter_dimension=0, tiled=True)
+    packed_attn = jnp.concatenate([summed.reshape(total_rows, query_width), side_block], axis=1)
+    count = lax.axis_size("ctx")
+    moved = lax.all_to_all(packed_attn, "ctx", 0, 0, tiled=True).reshape(count, row_share, -1)
+    shard_sums = moved[:, :, :query_width].reshape(count, row_share, groups, head_size)
+    shard_weights = moved[:, :, query_width : query_width + groups]
+    shard_high = moved[:, :, query_width + groups : query_width + 2 * groups]
+    top = jnp.max(shard_high, axis=0)
+    shrink = jnp.exp(shard_high - top[None])
+    total_sums = jnp.sum(shard_sums * shrink[:, :, :, None], axis=0)
+    total_weights = jnp.sum(shard_weights * shrink, axis=0)
     own_attended = (
-        (merged[:, :query_width].reshape(row_share, groups, head_size)
-         / merged[:, query_width : query_width + groups][:, :, None])
-        .reshape(row_share, query_width)
-        .astype(jnp.bfloat16)
+        (total_sums / total_weights[:, :, None]).reshape(row_share, query_width).astype(jnp.bfloat16)
     )
-    attended = lax.all_gather(own_attended, "ctx", axis=0, tiled=True)
-    return lax.psum_scatter(
-        jnp.dot(attended, out_weight, preferred_element_type=jnp.float32).astype(jnp.bfloat16),
-        ("sec", "head"),
-        scatter_dimension=0,
-        tiled=True,
-    )
+    attended = gather_rows(own_attended, "ctx")
+    projected_out = jnp.dot(attended, out_weight, preferred_element_type=jnp.float32)
+    return reduce_rows(projected_out, ("sec", "head")).astype(jnp.bfloat16)
 
 
 def solution(mesh):

time: 427 us -> 223 us (0.52)
  waiting for transfers between devices: 275 us -> 57.3 us
  starting transfers between devices: 0.17 us -> 16.2 us
  between operations: 13.3 us -> 0.25 us
  local copies, waits for them, and re-layouts: 5.52 us -> 16 us
  matrix products: 41.4 us -> 33.3 us
  blocking collectives: 68.1 us -> 74.2 us
    reduce_scatter x2 -> x0, waiting for transfers between devices: 108 us -> none  [the longest x1 78.4 us: body(): reduced = lax.psum_scatter(packed, 'ctx', scatter_dimension=0, tiled=True)]
    unnamed x6 -> x0, waiting for transfers between devices: 86.6 us -> none
    all_gather x2 -> x0, waiting for transfers between devices: 80.5 us -> none  [the longest x1 41.8 us: body(): attended = lax.all_gather(own_attended, 'ctx', axis=0, tiled=True)]
    all_to_all x0 -> x3, blocking collectives: none -> 74.2 us  [the longest x1 34.2 us: body(): lax.all_to_all(packed_attn, 'ctx', 0, 0, tiled=True)]
    pmax x1 -> x0, blocking collectives: 57.8 us -> none  [body(): highest = lax.pmax(local_high, 'ctx')]
    all_to_all x0 -> x2, waiting for transfers between devices: none -> 52.2 us  [the longest x1 40.1 us: reduce_rows(): moved = lax.all_to_all(value, axis, 0, 0, tiled=True)]
    all_to_all x0 -> x2, starting transfers between devices: none -> 12.7 us  [the longest x1 8.15 us: reduce_rows(): moved = lax.all_to_all(value, axis, 0, 0, tiled=True)]
    all_gather x1 -> x0, blocking collectives: 10.3 us -> none  [body(): gathered = lax.all_gather(proposal_rows, 'sec', axis=0, tiled=True)]
  transfers between devices with their start and end apart: 5 -> 3, of which waited for: 5 -> 3; matrix products, arithmetic and copies ran while one was open for 1% -> 2% of each run, Pallas kernels for 0% -> 0%
where the time goes in v2:
time: 223 us; the launch traced here: 222 us
  blocking collectives  74.2 us (33%)
  waiting for transfers between devices  57.3 us (26%)
  matrix products  33.3 us (15%)
  other arithmetic  24.9 us (11%)
  starting transfers between devices  16.2 us (7%)
  local copies, waits for them, and re-layouts  16 us (7%)
    all_to_all x1, waiting for transfers between devices, reduce_rows(): moved = lax.all_to_all(value, axis, 0, 0, tiled=True)  40.1 us
    all_to_all x1, blocking collectives, body(): lax.all_to_all(packed_attn, 'ctx', 0, 0, tiled=True)  34.2 us
    all_to_all x1, blocking collectives, reduce_rows(): moved = lax.all_to_all(value, axis, 0, 0, tiled=True)  23.2 us
    all_to_all x1, blocking collectives, gather_rows(): return lax.all_to_all(jnp.tile(value, (count, 1)), axis, 0, 0, tiled=True)  16.7 us
    reduce_sum x2, other arithmetic, body(): weight_sum = jnp.sum(weights, axis=2) + jnp.sum(tree_weights, axis=2)  15.3 us
    dot_general x1, matrix products, body(): jnp.einsum('rgd,td->rgt', grouped, keys, preferred_element_type=jnp.float32)  13.9 us
    dot_general x1, matrix products, body(): jnp.einsum('rgt,td->rgd', weights.astype(jnp.bfloat16), vals, preferred_e...  13.2 us
    all_to_all x1, waiting for transfers between devices, gather_rows(): return lax.all_to_all(jnp.tile(value, (count, 1)), axis, 0, 0, tiled=True)  12.1 us
  transfers between devices with their start and end apart: 3, of which 3 were waited for; matrix products, arithmetic and copies ran while one was open for 2% of the time, Pallas kernels for 0%

profile of v2, /device:TPU:1, one launch (start us, length us, event | category | flops | bytes accessed | tf_op | source)
XLA Modules:
  0.0 222.1 jit_solution(16857455429591466874)
XLA Ops:
  0.0 3.6 %collective-permute-start = (bf16[256,512]{1,0:T(8,128)(2,1)}, bf16[256,512]{1,0:T(8,128)(2,1)S(1)}, u32[]{:S(2)}, u32[]{:S(2)}) collective-permute-start(bf16[256,512]{1,0:T(8,128)(2,1)} %param.10), channel_id=1, source_target_pairs={{0,64},{64,0},{1,65},{65,1},{2,66},{66,2},{3,67},{67,3},{4,68},{68... | collective-permute-start | bytes 786440 | tf_op jit(solution)/shard_map/ppermute | solution.py:50
  3.6 0.7 convert_element_type.33
  4.3 5.1 %collective-permute-done = bf16[256,512]{1,0:T(8,128)(2,1)S(1)} collective-permute-done((bf16[256,512]{1,0:T(8,128)(2,1)}, bf16[256,512]{1,0:T(8,128)(2,1)S(1)}, u32[]{:S(2)}, u32[]{:S(2)}) %collective-permute-start) | collective-permute-done | bytes 262176 | tf_op jit(solution)/shard_map/ppermute | solution.py:50
  9.4 1.3 fusion.13
  10.7 0.1 broadcast_select_fusion
  10.8 2.4 %fusion.6 = f32[512,1280]{1,0:T(8,128)S(1)} fusion(bf16[512,128]{1,0:T(8,128)(2,1)} %bitcast.49, bf16[512,128]{1,0:T(8,128)(2,1)} %bitcast.50, bf16[512,1024]{1,0:T(8,128)(2,1)} %param.12, f32[512]{0:T(512)S(1)} %convert_element_type.33, bf16[256,512]{1,0:T(8,128)(2,1)S(1)} %collective-permute-done, bf16[256,512]{1,0:T(8,128)(2,1)} %param.10, pred[]{:T(512)S(6)} %eq.40), kind=kOutput, calls=%fused_computation.13 | convolution fusion | flops 678166528 | bytes 4458497 | tf_op jit(solution)/shard_map/dot_general | solution.py:65
  13.2 1.8 pad_maximum_fusion
  15.0 8.2 %all-to-all-start = ((f32[16,32,1408]{2,1,0:T(8,128)}), f32[16,32,1408]{2,1,0:T(8,128)}, u32[]{:S(2)}, u32[]{:S(2)}) async-start(f32[16,32,1408]{2,1,0:T(8,128)} %bitcast.41), calls=%async_computation | async-start | bytes 5767168 | tf_op jit(solution)/shard_map/all_to_all | solution.py:29
  23.1 0.0 copy-start.2
  23.2 40.1 %all-to-all-done = f32[16,32,1408]{2,1,0:T(8,128)} async-done(((f32[16,32,1408]{2,1,0:T(8,128)}), f32[16,32,1408]{2,1,0:T(8,128)}, u32[]{:S(2)}, u32[]{:S(2)}) %all-to-all-start) | async-done | bytes 2883616 | tf_op jit(solution)/shard_map/all_to_all | solution.py:29
  63.2 2.0 reduce_sum.64
  65.2 0.1 fusion.39
  65.3 0.1 fusion.35
  65.4 1.1 tile.4
  66.5 4.5 %all-to-all-start.1 = ((bf16[16,32,1024]{2,1,0:T(8,128)(2,1)}), bf16[16,32,1024]{2,1,0:T(8,128)(2,1)S(1)}, u32[]{:S(2)}, u32[]{:S(2)}) async-start(bf16[16,32,1024]{2,1,0:T(8,128)(2,1)} %tile.4), calls=%async_computation.1 | async-start | bytes 2097152 | tf_op jit(solution)/shard_map/all_to_all | solution.py:35
  71.1 0.1 broadcast_in_dim.78
  71.1 0.1 lt.23
  71.2 0.6 convolution_compare_fusion.2
  71.9 1.1 convolution_compare_fusion
  73.0 0.4 convolution_compare_fusion.3
  73.4 0.7 broadcast_compare_fusion
  74.0 12.1 %all-to-all-done.1 = bf16[16,32,1024]{2,1,0:T(8,128)(2,1)S(1)} async-done(((bf16[16,32,1024]{2,1,0:T(8,128)(2,1)}), bf16[16,32,1024]{2,1,0:T(8,128)(2,1)S(1)}, u32[]{:S(2)}, u32[]{:S(2)}) %all-to-all-start.1) | async-done | bytes 1048608 | tf_op jit(solution)/shard_map/all_to_all | solution.py:35
  86.2 0.3 copy.24
  86.4 0.5 select_reduce_fusion.1
  86.9 0.3 copy-done.1
  87.2 13.9 %select_reduce_fusion = (f32[512,8]{0,1:T(8,128)S(1)}, f32[512,8,2048]{2,0,1:T(8,128)}) fusion(pred[512,2048]{1,0:T(8,128)(4,1)S(1)} %broadcast_compare_fusion, bf16[2048,1,128]{2,0,1:T(8,128)(2,1)S(1)} %copy-done.1, bf16[512,8,128]{2,1,0:T(8,128)(2,1)S(1)} %bitcast.43), kind=kOutput, calls=%fused_computation.1 | convolution fusion | flops 2172645376 | bytes 36192256 | tf_op jit(solution)/shard_map/rgd,td->rgt/dot_general | solution.py:88
  101.2 0.1 copy.20
  101.3 0.1 fusion.27
  101.4 15.2 %fusion = f32[512,8]{0,1:T(8,128)S(1)} fusion(f32[512,8,2048]{2,0,1:T(8,128)} %get-tuple-element.8, f32[512,8]{0,1:T(8,128)S(1)} %max.11, pred[512,2048]{1,0:T(8,128)(4,1)S(1)} %broadcast_compare_fusion), kind=kLoop, calls=%fused_computation.2 | loop fusion | flops 33550336 | bytes 34635776 | tf_op jit(solution)/shard_map/reduce_sum | solution.py:99
  116.6 0.8 copy.23
  117.5 13.2 %fusion.2 = f32[512,8,128]{2,0,1:T(8,128)S(1)} fusion(f32[512,8,2048]{2,0,1:T(8,128)} %get-tuple-element.8, f32[512,8]{0,1:T(8,128)S(1)} %max.11, pred[512,2048]{1,0:T(8,128)(4,1)S(1)} %broadcast_compare_fusion, bf16[2048,1,128]{2,0,1:T(8,128)(2,1)} %param.17), kind=kOutput, calls=%fused_computation.4 | convolution fusion | flops 2181038080 | bytes 37240832 | tf_op jit(solution)/shard_map/rgt,td->rgd/dot_general | solution.py:100
  130.7 0.5 convolution_add_fusion
  131.2 2.6 %copy.19 = f32[512,8,128]{2,1,0:T(8,128)} copy(f32[512,8,128]{2,0,1:T(8,128)S(1)} %convolution_add_fusion) | data formatting | bytes 4194304 | tf_op jit(solution)/shard_map/add | solution.py:100
  133.7 1.7 concatenate.22
  135.5 0.7 broadcast_in_dim.88
  136.2 3.3 %concatenate.23 = f32[16,32,1152]{2,1,0:T(8,128)} concatenate(f32[16,32,1024]{2,1,0:T(8,128)S(1)} %concatenate.22, f32[16,32,8]{2,1,0:T(8,128)} %bitcast.46, f32[16,32,8]{2,1,0:T(8,128)S(1)} %bitcast.45, f32[16,32,112]{2,1,0:T(8,128)} %broadcast_in_dim.88), dimensions={2} | concatenate | bytes 4718592 | tf_op jit(solution)/shard_map/concatenate | solution.py:108
  139.5 34.2 %all_to_all.33 = f32[16,32,1152]{2,1,0:T(8,128)S(1)} all-to-all(f32[16,32,1152]{2,1,0:T(8,128)} %concatenate.23), channel_id=1, replica_groups=mesh['sec'=2,'head'=4,'ctx'=16] {'ctx'}, dimensions={0} | all-to-all | bytes 4718592 | tf_op jit(solution)/shard_map/all_to_all | solution.py:110
  173.8 0.1 slice_reduce_fusion
  173.9 0.1 fusion.30
  174.0 2.0 mul.65
  176.0 2.7 %mul.66 = f32[16,32,1024]{2,1,0:T(8,128)} reshape(f32[16,32,8,128]{3,2,1,0:T(8,128)} %mul.65) | data formatting | bytes 4194304 | tf_op jit(solution)/shard_map/mul | solution.py:116
  178.7 1.8 fusion.5
  180.5 0.1 div.23
  180.6 0.1 tile.5
  180.8 16.7 %all_to_all.34 = bf16[16,32,1024]{2,1,0:T(8,128)(2,1)S(1)} all-to-all(bf16[16,32,1024]{2,1,0:T(8,128)(2,1)S(1)} %tile.5), channel_id=1, replica_groups=mesh['sec'=2,'head'=4,'ctx'=16] {'ctx'}, dimensions={0} | all-to-all | bytes 2097152 | tf_op jit(solution)/shard_map/all_to_all | solution.py:35
  197.5 0.7 fusion.14
  198.2 23.2 %all_to_all.35 = f32[8,64,512]{2,1,0:T(8,128)S(1)} all-to-all(f32[8,64,512]{2,1,0:T(8,128)S(1)} %fusion.14), channel_id=1, replica_groups=mesh['sec'=2,'head'=4,'ctx'=16] {'sec','head'}, dimensions={0} | all-to-all | bytes 2097152 | tf_op jit(solution)/shard_map/all_to_all | solution.py:29
  221.4 0.7 reduce_sum.69
  (12 shorter events, 0.1 us)
Async XLA Ops:
  0.0 197.5 %copy-start = (bf16[1024,512]{1,0:T(8,128)(2,1)S(1)}, bf16[1024,512]{1,0:T(8,128)(2,1)}, u32[]{:S(2)}) copy-start(bf16[1024,512]{1,0:T(8,128)(2,1)} %param.15) | copy-start | bytes 3145732
  0.0 9.4 %collective-permute-start = (bf16[256,512]{1,0:T(8,128)(2,1)}, bf16[256,512]{1,0:T(8,128)(2,1)S(1)}, u32[]{:S(2)}, u32[]{:S(2)}) collective-permute-start(bf16[256,512]{1,0:T(8,128)(2,1)} %param.10), channel_id=1, source_target_pairs={{0,64},{64,0},{1,65},{65,1},{2,66},{66,2},{3,67},{67,3},{4,68},{68... | collective-permute-start | bytes 786440 | tf_op jit(solution)/shard_map/ppermute | solution.py:50
  15.0 48.2 %all-to-all-start = ((f32[16,32,1408]{2,1,0:T(8,128)}), f32[16,32,1408]{2,1,0:T(8,128)}, u32[]{:S(2)}, u32[]{:S(2)}) async-start(f32[16,32,1408]{2,1,0:T(8,128)} %bitcast.41), calls=%async_computation | async-start | bytes 5767168 | tf_op jit(solution)/shard_map/all_to_all | solution.py:29
  23.1 47.9 %copy-start.2 = (s32[32]{0:T(128)S(1)}, s32[32]{0:T(128)}, u32[]{:S(2)}) copy-start(s32[32]{0:T(128)} %param.18) | copy-start | bytes 388
  23.2 48.1 %copy-start.3 = (s32[512]{0:T(512)S(1)}, s32[512]{0:T(512)}, u32[]{:S(2)}) copy-start(s32[512]{0:T(512)} %param.19) | copy-start | bytes 6148
  66.5 19.6 %all-to-all-start.1 = ((bf16[16,32,1024]{2,1,0:T(8,128)(2,1)}), bf16[16,32,1024]{2,1,0:T(8,128)(2,1)S(1)}, u32[]{:S(2)}, u32[]{:S(2)}) async-start(bf16[16,32,1024]{2,1,0:T(8,128)(2,1)} %tile.4), calls=%async_computation.1 | async-start | bytes 2097152 | tf_op jit(solution)/shard_map/all_to_all | solution.py:35
  86.2 1.0 copy-start.1

commit v3 on v2

--- a/solution.py
+++ b/solution.py
@@ -94,6 +94,9 @@
         jnp.max(jnp.where(visible, scores, NEGATIVE), axis=2),
         jnp.max(jnp.where(tree_visible, tree_scores, NEGATIVE), axis=2),
     )
+    high_hi = lax.reduce_precision(local_high, exponent_bits=8, mantissa_bits=7)
+    high_lo = lax.reduce_precision(local_high - high_hi, exponent_bits=8, mantissa_bits=7)
+    local_high = high_hi + high_lo
     weights = jnp.where(visible, jnp.exp(scores - local_high[:, :, None]), 0.0)
     tree_weights = jnp.where(tree_visible, jnp.exp(tree_scores - local_high[:, :, None]), 0.0)
     weight_sum = jnp.sum(weights, axis=2) + jnp.sum(tree_weights, axis=2)
@@ -102,15 +105,22 @@
     ) + jnp.einsum(
         "rgt,td->rgd", tree_weights.astype(jnp.bfloat16), tree_vals, preferred_element_type=jnp.float32
     )
+    sum_hi = lax.reduce_precision(weight_sum, exponent_bits=8, mantissa_bits=7)
+    sum_lo = weight_sum - sum_hi
     side_block = jnp.concatenate(
-        [weight_sum, local_high, jnp.zeros((total_rows, 128 - 2 * groups), jnp.float32)], axis=1
+        [sum_hi, sum_lo, high_hi, high_lo, jnp.zeros((total_rows, 128 - 4 * groups), jnp.float32)],
+        axis=1,
+    ).astype(jnp.bfloat16)
+    packed_attn = jnp.concatenate(
+        [summed.reshape(total_rows, query_width).astype(jnp.bfloat16), side_block], axis=1
     )
-    packed_attn = jnp.concatenate([summed.reshape(total_rows, query_width), side_block], axis=1)
     count = lax.axis_size("ctx")
     moved = lax.all_to_all(packed_attn, "ctx", 0, 0, tiled=True).reshape(count, row_share, -1)
+    moved = moved.astype(jnp.float32)
     shard_sums = moved[:, :, :query_width].reshape(count, row_share, groups, head_size)
-    shard_weights = moved[:, :, query_width : query_width + groups]
-    shard_high = moved[:, :, query_width + groups : query_width + 2 * groups]
+    side = moved[:, :, query_width : query_width + 4 * groups].reshape(count, row_share, 4, groups)
+    shard_weights = side[:, :, 0] + side[:, :, 1]
+    shard_high = side[:, :, 2] + side[:, :, 3]
     top = jnp.max(shard_high, axis=0)
     shrink = jnp.exp(shard_high - top[None])
     total_sums = jnp.sum(shard_sums * shrink[:, :, :, None], axis=0)

time: 223 us -> 207 us (0.928)
  blocking collectives: 74.2 us -> 61.7 us
  local copies, waits for them, and re-layouts: 16 us -> 12 us
    all_to_all x1, blocking collectives: 34.2 us -> 21.8 us  [body(): lax.all_to_all(packed_attn, 'ctx', 0, 0, tiled=True)]
    add x1 -> x0, local copies, waits for them, and re-layouts: 2.57 us -> none  [body(): jnp.einsum('rgt,td->rgd', weights.astype(jnp.bfloat16), vals, preferred_e...]
    concatenate x2 -> x1, local copies, waits for them, and re-layouts: 5.03 us -> 2.57 us  [body(): jnp.concatenate([summed.reshape(total_rows, query_width).astype(jnp.bfloa...]
where the time goes in v3:
time: 207 us; the launch traced here: 206 us
  blocking collectives  61.7 us (30%)
  waiting for transfers between devices  57.3 us (28%)
  matrix products  33.2 us (16%)
  other arithmetic  25.5 us (12%)
  starting transfers between devices  16.2 us (8%)
  local copies, waits for them, and re-layouts  12 us (6%)
    all_to_all x1, waiting for transfers between devices, reduce_rows(): moved = lax.all_to_all(value, axis, 0, 0, tiled=True)  40.1 us
    all_to_all x1, blocking collectives, reduce_rows(): moved = lax.all_to_all(value, axis, 0, 0, tiled=True)  23 us
    all_to_all x1, blocking collectives, body(): lax.all_to_all(packed_attn, 'ctx', 0, 0, tiled=True)  21.8 us
    all_to_all x1, blocking collectives, gather_rows(): return lax.all_to_all(jnp.tile(value, (count, 1)), axis, 0, 0, tiled=True)  16.9 us
    reduce_sum x2, other arithmetic, body(): weight_sum = jnp.sum(weights, axis=2) + jnp.sum(tree_weights, axis=2)  15.4 us
    dot_general x1, matrix products, body(): jnp.einsum('rgd,td->rgt', grouped, keys, preferred_element_type=jnp.float32)  13.9 us
    dot_general x1, matrix products, body(): jnp.einsum('rgt,td->rgd', weights.astype(jnp.bfloat16), vals, preferred_e...  13.1 us
    all_to_all x1, waiting for transfers between devices, gather_rows(): return lax.all_to_all(jnp.tile(value, (count, 1)), axis, 0, 0, tiled=True)  12.1 us
  transfers between devices with their start and end apart: 3, of which 3 were waited for; matrix products, arithmetic and copies ran while one was open for 2% of the time, Pallas kernels for 0%

profile of v3, /device:TPU:1, one launch (start us, length us, event | category | flops | bytes accessed | tf_op | source)
XLA Modules:
  0.0 206.3 jit_solution(6645375528186441582)
XLA Ops:
  0.0 3.6 %collective-permute-start = (bf16[256,512]{1,0:T(8,128)(2,1)}, bf16[256,512]{1,0:T(8,128)(2,1)S(1)}, u32[]{:S(2)}, u32[]{:S(2)}) collective-permute-start(bf16[256,512]{1,0:T(8,128)(2,1)} %param.10), channel_id=1, source_target_pairs={{0,64},{64,0},{1,65},{65,1},{2,66},{66,2},{3,67},{67,3},{4,68},{68... | collective-permute-start | bytes 786440 | tf_op jit(solution)/shard_map/ppermute | solution.py:50
  3.6 0.7 convert_element_type.45
  4.3 5.1 %collective-permute-done = bf16[256,512]{1,0:T(8,128)(2,1)S(1)} collective-permute-done((bf16[256,512]{1,0:T(8,128)(2,1)}, bf16[256,512]{1,0:T(8,128)(2,1)S(1)}, u32[]{:S(2)}, u32[]{:S(2)}) %collective-permute-start) | collective-permute-done | bytes 262176 | tf_op jit(solution)/shard_map/ppermute | solution.py:50
  9.4 1.3 fusion.13
  10.7 0.1 broadcast_select_fusion
  10.8 2.4 %fusion.6 = f32[512,1280]{1,0:T(8,128)S(1)} fusion(bf16[512,128]{1,0:T(8,128)(2,1)} %bitcast.81, bf16[512,128]{1,0:T(8,128)(2,1)} %bitcast.82, bf16[512,1024]{1,0:T(8,128)(2,1)} %param.12, f32[512]{0:T(512)S(1)} %convert_element_type.45, bf16[256,512]{1,0:T(8,128)(2,1)S(1)} %collective-permute-done, bf16[256,512]{1,0:T(8,128)(2,1)} %param.10, pred[]{:T(512)S(6)} %eq.40), kind=kOutput, calls=%fused_computation.13 | convolution fusion | flops 678166528 | bytes 4458497 | tf_op jit(solution)/shard_map/dot_general | solution.py:65
  13.2 1.8 pad_maximum_fusion
  15.0 8.2 %all-to-all-start = ((f32[16,32,1408]{2,1,0:T(8,128)}), f32[16,32,1408]{2,1,0:T(8,128)}, u32[]{:S(2)}, u32[]{:S(2)}) async-start(f32[16,32,1408]{2,1,0:T(8,128)} %bitcast.72), calls=%async_computation | async-start | bytes 5767168 | tf_op jit(solution)/shard_map/all_to_all | solution.py:29
  23.2 40.1 %all-to-all-done = f32[16,32,1408]{2,1,0:T(8,128)} async-done(((f32[16,32,1408]{2,1,0:T(8,128)}), f32[16,32,1408]{2,1,0:T(8,128)}, u32[]{:S(2)}, u32[]{:S(2)}) %all-to-all-start) | async-done | bytes 2883616 | tf_op jit(solution)/shard_map/all_to_all | solution.py:29
  63.2 2.0 reduce_sum.64
  65.2 0.1 fusion.48
  65.3 0.1 fusion.36
  65.4 1.1 tile.4
  66.5 4.5 %all-to-all-start.1 = ((bf16[16,32,1024]{2,1,0:T(8,128)(2,1)}), bf16[16,32,1024]{2,1,0:T(8,128)(2,1)S(1)}, u32[]{:S(2)}, u32[]{:S(2)}) async-start(bf16[16,32,1024]{2,1,0:T(8,128)(2,1)} %tile.4), calls=%async_computation.1 | async-start | bytes 2097152 | tf_op jit(solution)/shard_map/all_to_all | solution.py:35
  71.2 0.6 convolution_compare_fusion.2
  71.9 1.1 convolution_compare_fusion
  73.0 0.4 convolution_compare_fusion.3
  73.4 0.7 broadcast_compare_fusion
  74.0 12.1 %all-to-all-done.1 = bf16[16,32,1024]{2,1,0:T(8,128)(2,1)S(1)} async-done(((bf16[16,32,1024]{2,1,0:T(8,128)(2,1)}), bf16[16,32,1024]{2,1,0:T(8,128)(2,1)S(1)}, u32[]{:S(2)}, u32[]{:S(2)}) %all-to-all-start.1) | async-done | bytes 1048608 | tf_op jit(solution)/shard_map/all_to_all | solution.py:35
  86.2 0.3 copy.64
  86.4 0.5 select_reduce_fusion.1
  86.9 0.3 copy-done.2
  87.2 13.9 %select_reduce_fusion = (f32[512,8]{0,1:T(8,128)S(1)}, f32[512,8,2048]{2,0,1:T(8,128)}) fusion(pred[512,2048]{1,0:T(8,128)(4,1)S(1)} %broadcast_compare_fusion, bf16[2048,1,128]{2,0,1:T(8,128)(2,1)S(1)} %copy-done.2, bf16[512,8,128]{2,1,0:T(8,128)(2,1)S(1)} %bitcast.74), kind=kOutput, calls=%fused_computation.1 | convolution fusion | flops 2172645376 | bytes 36192256 | tf_op jit(solution)/shard_map/rgd,td->rgt/dot_general | solution.py:88
  101.2 0.1 fusion.27
  101.3 15.2 %fusion = f32[512,8]{0,1:T(8,128)S(1)} fusion(f32[512,8,2048]{2,0,1:T(8,128)} %get-tuple-element.14, f32[512,8]{0,1:T(8,128)S(1)} %get-tuple-element.7, pred[512,2048]{1,0:T(8,128)(4,1)S(1)} %broadcast_compare_fusion), kind=kLoop, calls=%fused_computation.2 | loop fusion | flops 33550336 | bytes 34635776 | tf_op jit(solution)/shard_map/reduce_sum | solution.py:102
  116.6 13.1 %fusion.2 = f32[512,8,128]{2,0,1:T(8,128)S(1)} fusion(f32[512,8,2048]{2,0,1:T(8,128)} %get-tuple-element.14, f32[512,8]{0,1:T(8,128)S(1)} %get-tuple-element.7, pred[512,2048]{1,0:T(8,128)(4,1)S(1)} %broadcast_compare_fusion, bf16[2048,1,128]{2,0,1:T(8,128)(2,1)S(1)} %copy-done.4), kind=kOutput, calls=%fused_computation.4 | convolution fusion | flops 2181038080 | bytes 37240832 | tf_op jit(solution)/shard_map/rgt,td->rgd/dot_general | solution.py:103
  129.6 0.5 add_convert_fusion
  130.1 0.7 copy.50
  130.8 0.5 convert_element_type.50
  131.4 0.1 copy.55
  131.6 0.1 copy.54
  131.7 0.1 copy.53
  131.8 0.7 fusion.30
  132.6 0.7 broadcast_in_dim.88
  133.3 2.6 %concatenate.24 = bf16[16,32,1152]{2,1,0:T(8,128)(2,1)S(1)} concatenate(bf16[16,32,1024]{2,1,0:T(8,128)(2,1)S(1)} %convert_element_type.50, bf16[16,32,8]{2,1,0:T(8,128)(2,1)S(1)} %copy.54, bf16[16,32,8]{2,1,0:T(8,128)(2,1)S(1)} %copy.55, bf16[16,32,8]{2,1,0:T(8,128)(2,1)} %get-tuple-element.10, bf16[16,32,8]{2,1,0:T(8,128)(2,1)} %get-tuple-element.9, ...), dimensions={2} | concatenate | bytes 2359296 | tf_op jit(solution)/shard_map/concatenate | solution.py:114
  135.8 21.8 %all_to_all.33 = bf16[16,32,1152]{2,1,0:T(8,128)(2,1)S(1)} all-to-all(bf16[16,32,1152]{2,1,0:T(8,128)(2,1)S(1)} %concatenate.24), channel_id=1, replica_groups=mesh['sec'=2,'head'=4,'ctx'=16] {'ctx'}, dimensions={0} | all-to-all | bytes 2359296 | tf_op jit(solution)/shard_map/all_to_all | solution.py:118
  157.6 1.0 copy-done.1
  158.7 0.1 copy.56
  159.0 0.1 copy.59
  159.1 2.0 mul.65
  161.1 1.7 mul.66
  162.8 1.5 convert_element_type.51
  164.3 0.4 fusion.5
  164.8 0.1 tile.5
  165.0 16.9 %all_to_all.34 = bf16[16,32,1024]{2,1,0:T(8,128)(2,1)S(1)} all-to-all(bf16[16,32,1024]{2,1,0:T(8,128)(2,1)S(1)} %tile.5), channel_id=1, replica_groups=mesh['sec'=2,'head'=4,'ctx'=16] {'ctx'}, dimensions={0} | all-to-all | bytes 2097152 | tf_op jit(solution)/shard_map/all_to_all | solution.py:35
  181.9 0.7 fusion.14
  182.6 23.0 %all_to_all.35 = f32[8,64,512]{2,1,0:T(8,128)S(1)} all-to-all(f32[8,64,512]{2,1,0:T(8,128)S(1)} %fusion.14), channel_id=1, replica_groups=mesh['sec'=2,'head'=4,'ctx'=16] {'sec','head'}, dimensions={0} | all-to-all | bytes 2097152 | tf_op jit(solution)/shard_map/all_to_all | solution.py:29
  205.6 0.7 reduce_sum.69
  (25 shorter events, 0.6 us)
Async XLA Ops:
  0.0 181.9 %copy-start = (bf16[1024,512]{1,0:T(8,128)(2,1)S(1)}, bf16[1024,512]{1,0:T(8,128)(2,1)}, u32[]{:S(2)}) copy-start(bf16[1024,512]{1,0:T(8,128)(2,1)} %param.15) | copy-start | bytes 3145732
  0.0 9.4 %collective-permute-start = (bf16[256,512]{1,0:T(8,128)(2,1)}, bf16[256,512]{1,0:T(8,128)(2,1)S(1)}, u32[]{:S(2)}, u32[]{:S(2)}) collective-permute-start(bf16[256,512]{1,0:T(8,128)(2,1)} %param.10), channel_id=1, source_target_pairs={{0,64},{64,0},{1,65},{65,1},{2,66},{66,2},{3,67},{67,3},{4,68},{68... | collective-permute-start | bytes 786440 | tf_op jit(solution)/shard_map/ppermute | solution.py:50
  15.0 48.2 %all-to-all-start = ((f32[16,32,1408]{2,1,0:T(8,128)}), f32[16,32,1408]{2,1,0:T(8,128)}, u32[]{:S(2)}, u32[]{:S(2)}) async-start(f32[16,32,1408]{2,1,0:T(8,128)} %bitcast.72), calls=%async_computation | async-start | bytes 5767168 | tf_op jit(solution)/shard_map/all_to_all | solution.py:29
  23.1 47.9 %copy-start.3 = (s32[32]{0:T(128)S(1)}, s32[32]{0:T(128)}, u32[]{:S(2)}) copy-start(s32[32]{0:T(128)} %param.18) | copy-start | bytes 388
  23.2 48.1 %copy-start.5 = (s32[512]{0:T(512)S(1)}, s32[512]{0:T(512)}, u32[]{:S(2)}) copy-start(s32[512]{0:T(512)} %param.19) | copy-start | bytes 6148
  66.5 19.6 %all-to-all-start.1 = ((bf16[16,32,1024]{2,1,0:T(8,128)(2,1)}), bf16[16,32,1024]{2,1,0:T(8,128)(2,1)S(1)}, u32[]{:S(2)}, u32[]{:S(2)}) async-start(bf16[16,32,1024]{2,1,0:T(8,128)(2,1)} %tile.4), calls=%async_computation.1 | async-start | bytes 2097152 | tf_op jit(solution)/shard_map/all_to_all | solution.py:35
  86.2 1.0 copy-start.2
  101.3 15.3 %copy-start.4 = (bf16[2048,1,128]{2,0,1:T(8,128)(2,1)S(1)}, bf16[2048,1,128]{2,0,1:T(8,128)(2,1)}, u32[]{:S(2)}) copy-start(bf16[2048,1,128]{2,0,1:T(8,128)(2,1)} %param.17) | copy-start | bytes 1572868
  157.6 1.0 copy-start.1

commit v4 on v3

--- a/solution.py
+++ b/solution.py
@@ -3,6 +3,8 @@
 import jax
 import jax.numpy as jnp
 from jax import lax
+from jax.experimental import pallas as pl
+from jax.experimental.pallas import tpu as pltpu
 from jax.sharding import PartitionSpec as P
 
 D = 8192
@@ -22,6 +24,79 @@
         reach = (jnp.dot(reach, reach, preferred_element_type=jnp.float32) > 0).astype(jnp.bfloat16)
     columns = lax.dynamic_slice_in_dim(reach, column_offset, column_amount, 1)
     return jnp.dot(reach, columns, preferred_element_type=jnp.float32) > 0
+
+
+def split_three(value):
+    high = lax.reduce_precision(value, exponent_bits=8, mantissa_bits=7)
+    rest = value - high
+    middle = lax.reduce_precision(rest, exponent_bits=8, mantissa_bits=7)
+    return high, middle, rest - middle
+
+
+def attend_kernel(
+    query_ref, key_ref, value_ref, length_ref, tree_key_ref, tree_value_ref, tree_mask_ref,
+    out_ref, high_ref, total_ref, *, factor,
+):
+    query = query_ref[...]
+    scores = lax.dot_general(
+        query, key_ref[...], (((1,), (1,)), ((), ())), preferred_element_type=jnp.float32
+    ) * factor
+    place = lax.broadcasted_iota(jnp.int32, scores.shape, 1)
+    visible = place < length_ref[...]
+    scores = jnp.where(visible, scores, NEGATIVE)
+    tree_scores = lax.dot_general(
+        query, tree_key_ref[...], (((1,), (1,)), ((), ())), preferred_element_type=jnp.float32
+    ) * factor
+    tree_visible = tree_mask_ref[...] > 0
+    tree_scores = jnp.where(tree_visible, tree_scores, NEGATIVE)
+    high = jnp.maximum(
+        jnp.max(scores, axis=1, keepdims=True), jnp.max(tree_scores, axis=1, keepdims=True)
+    )
+    weights = jnp.where(visible, jnp.exp(scores - high), 0.0)
+    tree_weights = jnp.where(tree_visible, jnp.exp(tree_scores - high), 0.0)
+    total_ref[...] = jnp.sum(weights, axis=1, keepdims=True) + jnp.sum(
+        tree_weights, axis=1, keepdims=True
+    )
+    high_ref[...] = high
+    out_ref[...] = (
+        jnp.dot(weights.astype(jnp.bfloat16), value_ref[...], preferred_element_type=jnp.float32)
+        + jnp.dot(
+            tree_weights.astype(jnp.bfloat16), tree_value_ref[...],
+            preferred_element_type=jnp.float32,
+        )
+    ).astype(jnp.bfloat16)
+
+
+def attend(query, keys, vals, lengths, tree_keys, tree_vals, tree_mask, factor, block=512):
+    amount, head_size = query.shape
+    span = keys.shape[0]
+    tree_amount = tree_keys.shape[0]
+    whole = lambda i: (0, 0)
+    rows = lambda i: (i, 0)
+    return pl.pallas_call(
+        lambda *refs: attend_kernel(*refs, factor=factor),
+        out_shape=(
+            jax.ShapeDtypeStruct((amount, head_size), jnp.bfloat16),
+            jax.ShapeDtypeStruct((amount, 1), jnp.float32),
+            jax.ShapeDtypeStruct((amount, 1), jnp.float32),
+        ),
+        grid=(amount // block,),
+        in_specs=[
+            pl.BlockSpec((block, head_size), rows),
+            pl.BlockSpec((span, head_size), whole),
+            pl.BlockSpec((span, head_size), whole),
+            pl.BlockSpec((block, 1), rows),
+            pl.BlockSpec((tree_amount, head_size), whole),
+            pl.BlockSpec((tree_amount, head_size), whole),
+            pl.BlockSpec((block, tree_amount), rows),
+        ],
+        out_specs=(
+            pl.BlockSpec((block, head_size), rows),
+            pl.BlockSpec((block, 1), rows),
+            pl.BlockSpec((block, 1), rows),
+        ),
+        compiler_params=pltpu.CompilerParams(dimension_semantics=("arbitrary",)),
+    )(query, keys, vals, lengths, tree_keys, tree_vals, tree_mask)
 
 
 def reduce_rows(value, axis):
@@ -81,46 +156,31 @@
     vals = context_values[:, 0, :]
     span = keys.shape[0]
     factor = 1.0 / math.sqrt(head_size)
-    grouped = queries.reshape(total_rows, groups, head_size)
     lengths_rows = jnp.repeat(prefix_lengths, PROPOSALS)
-    positions = position * span + jnp.arange(span, dtype=jnp.int32)
-    visible = (positions[None, :] < lengths_rows[:, None])[:, None, :]
-    scores = jnp.einsum("rgd,td->rgt", grouped, keys, preferred_element_type=jnp.float32) * factor
-    tree_visible = ancestry_columns(parents, position * row_share, row_share)[:, None, :]
-    tree_scores = (
-        jnp.einsum("rgd,td->rgt", grouped, tree_keys, preferred_element_type=jnp.float32) * factor
-    )
-    local_high = jnp.maximum(
-        jnp.max(jnp.where(visible, scores, NEGATIVE), axis=2),
-        jnp.max(jnp.where(tree_visible, tree_scores, NEGATIVE), axis=2),
-    )
-    high_hi = lax.reduce_precision(local_high, exponent_bits=8, mantissa_bits=7)
-    high_lo = lax.reduce_precision(local_high - high_hi, exponent_bits=8, mantissa_bits=7)
-    local_high = high_hi + high_lo
-    weights = jnp.where(visible, jnp.exp(scores - local_high[:, :, None]), 0.0)
-    tree_weights = jnp.where(tree_visible, jnp.exp(tree_scores - local_high[:, :, None]), 0.0)
-    weight_sum = jnp.sum(weights, axis=2) + jnp.sum(tree_weights, axis=2)
-    summed = jnp.einsum(
-        "rgt,td->rgd", weights.astype(jnp.bfloat16), vals, preferred_element_type=jnp.float32
-    ) + jnp.einsum(
-        "rgt,td->rgd", tree_weights.astype(jnp.bfloat16), tree_vals, preferred_element_type=jnp.float32
-    )
+    lengths_query = jnp.repeat(lengths_rows - position * span, groups)[:, None]
+    tree_mask = jnp.repeat(
+        ancestry_columns(parents, position * row_share, row_share).astype(jnp.bfloat16), groups, axis=0
+    )
+    summed, high, weight_sum = attend(
+        queries.reshape(total_rows * groups, head_size), keys, vals, lengths_query,
+        tree_keys, tree_vals, tree_mask, factor,
+    )
+    high = high.reshape(total_rows, groups)
+    weight_sum = weight_sum.reshape(total_rows, groups)
     sum_hi = lax.reduce_precision(weight_sum, exponent_bits=8, mantissa_bits=7)
     sum_lo = weight_sum - sum_hi
     side_block = jnp.concatenate(
-        [sum_hi, sum_lo, high_hi, high_lo, jnp.zeros((total_rows, 128 - 4 * groups), jnp.float32)],
+        [sum_hi, sum_lo, *split_three(high), jnp.zeros((total_rows, 128 - 5 * groups), jnp.float32)],
         axis=1,
     ).astype(jnp.bfloat16)
-    packed_attn = jnp.concatenate(
-        [summed.reshape(total_rows, query_width).astype(jnp.bfloat16), side_block], axis=1
-    )
+    packed_attn = jnp.concatenate([summed.reshape(total_rows, query_width), side_block], axis=1)
     count = lax.axis_size("ctx")
     moved = lax.all_to_all(packed_attn, "ctx", 0, 0, tiled=True).reshape(count, row_share, -1)
     moved = moved.astype(jnp.float32)
     shard_sums = moved[:, :, :query_width].reshape(count, row_share, groups, head_size)
-    side = moved[:, :, query_width : query_width + 4 * groups].reshape(count, row_share, 4, groups)
+    side = moved[:, :, query_width : query_width + 5 * groups].reshape(count, row_share, 5, groups)
     shard_weights = side[:, :, 0] + side[:, :, 1]
-    shard_high = side[:, :, 2] + side[:, :, 3]
+    shard_high = side[:, :, 2] + side[:, :, 3] + side[:, :, 4]
     top = jnp.max(shard_high, axis=0)
     shrink = jnp.exp(shard_high - top[None])
     total_sums = jnp.sum(shard_sums * shrink[:, :, :, None], axis=0)

time: 207 us -> 203 us (0.981)
  Pallas kernels: 0 us -> 32.4 us
  matrix products: 33.2 us -> 5.21 us
  other arithmetic: 25.5 us -> 16.2 us
  local copies, waits for them, and re-layouts: 12 us -> 16.2 us
  waiting for transfers between devices: 57.3 us -> 54.1 us
    pallas_call x0 -> x1, Pallas kernels: none -> 32.4 us  [attend(): pl.pallas_call(lambda *refs: attend_kernel(*refs, factor=factor), out_sha...]
    dot_general x4 -> x0, matrix products: 28 us -> none  [the longest x1 13.9 us: body(): jnp.einsum('rgd,td->rgt', grouped, keys, preferred_element_type=jnp.float32)]
    reduce_sum x2 -> x0, other arithmetic: 15.4 us -> none  [body(): weight_sum = jnp.sum(weights, axis=2) + jnp.sum(tree_weights, axis=2)]
    all_to_all x1, waiting for transfers between devices: 40.1 us -> 35.5 us  [reduce_rows(): moved = lax.all_to_all(value, axis, 0, 0, tiled=True)]
    pallas_call x0 -> x2, other arithmetic: none -> 4.4 us  [attend(): pl.pallas_call(lambda *refs: attend_kernel(*refs, factor=factor), out_sha...]
    mul x2 -> x0, local copies, waits for them, and re-layouts: 3.68 us -> none  [body(): total_sums = jnp.sum(shard_sums * shrink[:, :, :, None], axis=0)]
    all_to_all x0 -> x1, local copies, waits for them, and re-layouts: none -> 3.28 us  [body(): lax.all_to_all(packed_attn, 'ctx', 0, 0, tiled=True)]
    reshape x0 -> x6, local copies, waits for them, and re-layouts: none -> 2.87 us  [the longest x1 1.28 us: body(): queries.reshape(total_rows * groups, head_size)]
  transfers between devices with their start and end apart: 3 -> 3, of which waited for: 3 -> 3; matrix products, arithmetic and copies ran while one was open for 2% -> 3% of each run, Pallas kernels for 0% -> 0%
where the time goes in v4:
time: 203 us; the launch traced here: 202 us
  blocking collectives  61.7 us (30%)
  waiting for transfers between devices  54.1 us (27%)
  Pallas kernels  32.4 us (16%)
  starting transfers between devices  16.4 us (8%)
  local copies, waits for them, and re-layouts  16.2 us (8%)
  other arithmetic  16.2 us (8%)
  matrix products  5.21 us (3%)
    all_to_all x1, waiting for transfers between devices, reduce_rows(): moved = lax.all_to_all(value, axis, 0, 0, tiled=True)  35.5 us
    pallas_call x1, Pallas kernels, attend(): pl.pallas_call(lambda *refs: attend_kernel(*refs, factor=factor), out_sha...  32.4 us
    all_to_all x1, blocking collectives, reduce_rows(): moved = lax.all_to_all(value, axis, 0, 0, tiled=True)  23 us
    all_to_all x1, blocking collectives, body(): lax.all_to_all(packed_attn, 'ctx', 0, 0, tiled=True)  21.8 us
    all_to_all x1, blocking collectives, gather_rows(): return lax.all_to_all(jnp.tile(value, (count, 1)), axis, 0, 0, tiled=True)  17 us
    all_to_all x1, waiting for transfers between devices, gather_rows(): return lax.all_to_all(jnp.tile(value, (count, 1)), axis, 0, 0, tiled=True)  13.4 us
    all_to_all x1, starting transfers between devices, reduce_rows(): moved = lax.all_to_all(value, axis, 0, 0, tiled=True)  8.28 us
    ppermute x1, waiting for transfers between devices, body(): other_rows = lax.ppermute(proposal_rows, 'sec', [(0, 1), (1, 0)])  5.14 us
  transfers between devices with their start and end apart: 3, of which 3 were waited for; matrix products, arithmetic and copies ran while one was open for 3% of the time, Pallas kernels for 0%

profile of v4, /device:TPU:1, one launch (start us, length us, event | category | flops | bytes accessed | tf_op | source)
XLA Modules:
  0.0 202.5 jit_solution(2280236593942916496)
XLA Ops:
  0.0 3.6 %collective-permute-start = (bf16[256,512]{1,0:T(8,128)(2,1)}, bf16[256,512]{1,0:T(8,128)(2,1)S(1)}, u32[]{:S(2)}, u32[]{:S(2)}) collective-permute-start(bf16[256,512]{1,0:T(8,128)(2,1)} %param.10), channel_id=1, source_target_pairs={{0,64},{64,0},{1,65},{65,1},{2,66},{66,2},{3,67},{67,3},{4,68},{68... | collective-permute-start | bytes 786440 | tf_op jit(solution)/shard_map/ppermute | solution.py:125
  3.6 0.7 convert_element_type.35
  4.3 5.1 %collective-permute-done = bf16[256,512]{1,0:T(8,128)(2,1)S(1)} collective-permute-done((bf16[256,512]{1,0:T(8,128)(2,1)}, bf16[256,512]{1,0:T(8,128)(2,1)S(1)}, u32[]{:S(2)}, u32[]{:S(2)}) %collective-permute-start) | collective-permute-done | bytes 262176 | tf_op jit(solution)/shard_map/ppermute | solution.py:125
  9.4 1.3 fusion.9
  10.7 0.1 broadcast_select_fusion
  10.8 2.4 %fusion.1 = f32[512,1280]{1,0:T(8,128)S(1)} fusion(bf16[512,128]{1,0:T(8,128)(2,1)} %bitcast.67, bf16[512,128]{1,0:T(8,128)(2,1)} %bitcast.68, bf16[512,1024]{1,0:T(8,128)(2,1)} %param.12, f32[512]{0:T(512)S(1)} %convert_element_type.35, bf16[256,512]{1,0:T(8,128)(2,1)S(1)} %collective-permute-done, bf16[256,512]{1,0:T(8,128)(2,1)} %param.10, pred[]{:T(512)S(6)} %eq.40), kind=kOutput, calls=%fused_computation.5 | convolution fusion | flops 678166528 | bytes 4458497 | tf_op jit(solution)/shard_map/dot_general | solution.py:140
  13.2 1.8 pad_maximum_fusion
  15.0 8.3 %all-to-all-start = ((f32[16,32,1408]{2,1,0:T(8,128)}), f32[16,32,1408]{2,1,0:T(8,128)}, u32[]{:S(2)}, u32[]{:S(2)}) async-start(f32[16,32,1408]{2,1,0:T(8,128)} %bitcast.63), calls=%async_computation | async-start | bytes 5767168 | tf_op jit(solution)/shard_map/all_to_all | solution.py:104
  23.4 0.1 sub.37
  23.5 0.6 convolution_compare_fusion.2
  24.1 1.1 convolution_compare_fusion
  25.2 0.4 fusion.7
  25.6 0.1 copy.35
  25.7 0.1 broadcast_in_dim.47
  25.9 2.0 broadcast_in_dim_reshape.4.refs_3_
  27.8 35.5 %all-to-all-done = f32[16,32,1408]{2,1,0:T(8,128)} async-done(((f32[16,32,1408]{2,1,0:T(8,128)}), f32[16,32,1408]{2,1,0:T(8,128)}, u32[]{:S(2)}, u32[]{:S(2)}) %all-to-all-start) | async-done | bytes 2883616 | tf_op jit(solution)/shard_map/all_to_all | solution.py:104
  63.4 2.0 reduce_sum.46
  65.3 0.1 fusion.31
  65.4 0.1 fusion.21
  65.5 1.1 tile.4
  66.7 4.5 %all-to-all-start.1 = ((bf16[16,32,1024]{2,1,0:T(8,128)(2,1)}), bf16[16,32,1024]{2,1,0:T(8,128)(2,1)S(1)}, u32[]{:S(2)}, u32[]{:S(2)}) async-start(bf16[16,32,1024]{2,1,0:T(8,128)(2,1)} %tile.4), calls=%async_computation.1 | async-start | bytes 2097152 | tf_op jit(solution)/shard_map/all_to_all | solution.py:110
  71.2 1.1 broadcast_bitcast_fusion.refs_6_
  72.3 0.6 fusion.37
  72.9 13.4 %all-to-all-done.1 = bf16[16,32,1024]{2,1,0:T(8,128)(2,1)S(1)} async-done(((bf16[16,32,1024]{2,1,0:T(8,128)(2,1)}), bf16[16,32,1024]{2,1,0:T(8,128)(2,1)S(1)}, u32[]{:S(2)}, u32[]{:S(2)}) %all-to-all-start.1) | async-done | bytes 1048608 | tf_op jit(solution)/shard_map/all_to_all | solution.py:110
  86.3 1.3 reshape.105.refs_0_
  87.6 32.4 %shard_map.100 = (bf16[4096,128]{1,0:T(8,128)(2,1)}, f32[4096,1]{1,0:T(8,128)}, f32[4096,1]{1,0:T(8,128)}) custom-call(bf16[4096,128]{1,0:T(8,128)(2,1)} %reshape.105.refs_0_, bf16[2048,128]{1,0:T(8,128)(2,1)} %bitcast.65, bf16[2048,128]{1,0:T(8,128)(2,1)} %bitcast.66, s32[4096,1]{1,0:T(8,128)} %broadcast_in_dim_reshape.4.refs_3_, ...), custom_call_target="tpu_custom_call" | custom-call | tf_op jit(solution)/shard_map/pallas_call | solution.py:76
  120.0 1.5 concatenate.26
  121.5 2.2 %reduce.5 = f32[4096]{0:T(1024)S(1)} reduce(f32[4096,1]{1,0:T(8,128)} %get-tuple-element.9, f32[]{:T(128)} %constant.37), dimensions={1}, to_apply=%get-tuple-element.9.reduce_sub_computation | reduce | bytes 32772 | tf_op jit(solution)/shard_map/pallas_call | solution.py:76
  123.7 2.2 %reduce.6 = f32[4096]{0:T(1024)S(1)} reduce(f32[4096,1]{1,0:T(8,128)} %get-tuple-element.10, f32[]{:T(128)} %constant.37), dimensions={1}, to_apply=%get-tuple-element.10.reduce_sub_computation | reduce | bytes 32772 | tf_op jit(solution)/shard_map/pallas_call | solution.py:76
  125.9 0.2 reshape.108
  126.1 0.1 copy.37
  126.3 0.1 copy.41
  126.4 0.1 copy.40
  126.5 0.8 copy.39
  127.3 0.2 reshape.107
  127.5 0.7 fusion.19
  128.2 0.7 broadcast_in_dim.49
  128.9 2.6 %concatenate.27 = bf16[16,32,1152]{2,1,0:T(8,128)(2,1)S(1)} concatenate(bf16[16,32,1024]{2,1,0:T(8,128)(2,1)S(1)} %concatenate.26, bf16[16,32,8]{2,1,0:T(8,128)(2,1)} %get-tuple-element.14, bf16[16,32,8]{2,1,0:T(8,128)(2,1)} %get-tuple-element.13, bf16[16,32,8]{2,1,0:T(8,128)(2,1)} %copy.39, bf16[16,32,8]{2,1,0:T(8,128)(2,1)S(1)} %copy.40, bf16[16,32,8]{2,1,0:T(8,128)(2,1)S(1)} %copy.41, ...), dimensions={2} | concatenate | bytes 2359296 | tf_op jit(solution)/shard_map/concatenate | solution.py:176
  131.4 21.8 %all_to_all.33 = bf16[16,32,1152]{2,1,0:T(8,128)(2,1)S(1)} all-to-all(bf16[16,32,1152]{2,1,0:T(8,128)(2,1)S(1)} %concatenate.27), channel_id=1, replica_groups=mesh['sec'=2,'head'=4,'ctx'=16] {'ctx'}, dimensions={0} | all-to-all | bytes 2359296 | tf_op jit(solution)/shard_map/all_to_all | solution.py:178
  153.2 3.3 %copy.42 = bf16[16,32,1152]{1,2,0:T(8,128)(2,1)} copy(bf16[16,32,1152]{2,1,0:T(8,128)(2,1)S(1)} %all_to_all.33) | data formatting | bytes 2359296 | tf_op jit(solution)/shard_map/all_to_all | solution.py:178
  156.5 3.3 %convert_element_type.38 = f32[16,32,1152]{1,2,0:T(8,128)S(1)} convert(bf16[16,32,1152]{1,2,0:T(8,128)(2,1)} %copy.42) | non-fusion elementwise | flops 589824 | bytes 3538944 | tf_op jit(solution)/shard_map/convert_element_type | solution.py:179
  159.9 0.9 fusion
  160.8 0.1 copy.46
  161.0 0.1 tile.5
  161.1 17.0 %all_to_all.34 = bf16[16,32,1024]{2,1,0:T(8,128)(2,1)S(1)} all-to-all(bf16[16,32,1024]{2,1,0:T(8,128)(2,1)S(1)} %tile.5), channel_id=1, replica_groups=mesh['sec'=2,'head'=4,'ctx'=16] {'ctx'}, dimensions={0} | all-to-all | bytes 2097152 | tf_op jit(solution)/shard_map/all_to_all | solution.py:110
  178.0 0.7 fusion.10
  178.8 23.0 %all_to_all.35 = f32[8,64,512]{2,1,0:T(8,128)S(1)} all-to-all(f32[8,64,512]{2,1,0:T(8,128)S(1)} %fusion.10), channel_id=1, replica_groups=mesh['sec'=2,'head'=4,'ctx'=16] {'sec','head'}, dimensions={0} | all-to-all | bytes 2097152 | tf_op jit(solution)/shard_map/all_to_all | solution.py:104
  201.7 0.7 reduce_sum.49
  (15 shorter events, 0.3 us)
Async XLA Ops:
  0.0 178.0 %copy-start = (bf16[1024,512]{1,0:T(8,128)(2,1)S(1)}, bf16[1024,512]{1,0:T(8,128)(2,1)}, u32[]{:S(2)}) copy-start(bf16[1024,512]{1,0:T(8,128)(2,1)} %param.15) | copy-start | bytes 3145732
  0.0 9.4 %collective-permute-start = (bf16[256,512]{1,0:T(8,128)(2,1)}, bf16[256,512]{1,0:T(8,128)(2,1)S(1)}, u32[]{:S(2)}, u32[]{:S(2)}) collective-permute-start(bf16[256,512]{1,0:T(8,128)(2,1)} %param.10), channel_id=1, source_target_pairs={{0,64},{64,0},{1,65},{65,1},{2,66},{66,2},{3,67},{67,3},{4,68},{68... | collective-permute-start | bytes 786440 | tf_op jit(solution)/shard_map/ppermute | solution.py:125
  15.0 8.3 %copy-start.2 = (s32[32]{0:T(128)S(1)}, s32[32]{0:T(128)}, u32[]{:S(2)}) copy-start(s32[32]{0:T(128)} %param.18) | copy-start | bytes 388
  15.0 8.5 %copy-start.1 = (s32[512]{0:T(512)S(1)}, s32[512]{0:T(512)}, u32[]{:S(2)}) copy-start(s32[512]{0:T(512)} %param.19) | copy-start | bytes 6148
  15.0 48.4 %all-to-all-start = ((f32[16,32,1408]{2,1,0:T(8,128)}), f32[16,32,1408]{2,1,0:T(8,128)}, u32[]{:S(2)}, u32[]{:S(2)}) async-start(f32[16,32,1408]{2,1,0:T(8,128)} %bitcast.63), calls=%async_computation | async-start | bytes 5767168 | tf_op jit(solution)/shard_map/all_to_all | solution.py:104
  66.7 19.6 %all-to-all-start.1 = ((bf16[16,32,1024]{2,1,0:T(8,128)(2,1)}), bf16[16,32,1024]{2,1,0:T(8,128)(2,1)S(1)}, u32[]{:S(2)}, u32[]{:S(2)}) async-start(bf16[16,32,1024]{2,1,0:T(8,128)(2,1)} %tile.4), calls=%async_computation.1 | async-start | bytes 2097152 | tf_op jit(solution)/shard_map/all_to_all | solution.py:110

commit v5 on v4

--- a/solution.py
+++ b/solution.py
@@ -34,69 +34,85 @@
 
 
 def attend_kernel(
-    query_ref, key_ref, value_ref, length_ref, tree_key_ref, tree_value_ref, tree_mask_ref,
-    out_ref, high_ref, total_ref, *, factor,
+    query_ref, key_ref, value_ref, bias_ref, tree_key_ref, tree_value_ref, tree_mask_ref,
+    out_ref, side_ref, *, factor, groups, per_particle,
 ):
-    query = query_ref[...]
-    scores = lax.dot_general(
-        query, key_ref[...], (((1,), (1,)), ((), ())), preferred_element_type=jnp.float32
-    ) * factor
-    place = lax.broadcasted_iota(jnp.int32, scores.shape, 1)
-    visible = place < length_ref[...]
-    scores = jnp.where(visible, scores, NEGATIVE)
-    tree_scores = lax.dot_general(
-        query, tree_key_ref[...], (((1,), (1,)), ((), ())), preferred_element_type=jnp.float32
-    ) * factor
+    keys = key_ref[...]
+    vals = value_ref[...]
+    tree_keys = tree_key_ref[...]
+    tree_vals = tree_value_ref[...]
+    bias = bias_ref[...]
     tree_visible = tree_mask_ref[...] > 0
-    tree_scores = jnp.where(tree_visible, tree_scores, NEGATIVE)
-    high = jnp.maximum(
-        jnp.max(scores, axis=1, keepdims=True), jnp.max(tree_scores, axis=1, keepdims=True)
-    )
-    weights = jnp.where(visible, jnp.exp(scores - high), 0.0)
-    tree_weights = jnp.where(tree_visible, jnp.exp(tree_scores - high), 0.0)
-    total_ref[...] = jnp.sum(weights, axis=1, keepdims=True) + jnp.sum(
-        tree_weights, axis=1, keepdims=True
-    )
-    high_ref[...] = high
-    out_ref[...] = (
-        jnp.dot(weights.astype(jnp.bfloat16), value_ref[...], preferred_element_type=jnp.float32)
-        + jnp.dot(
-            tree_weights.astype(jnp.bfloat16), tree_value_ref[...],
-            preferred_element_type=jnp.float32,
+    amount = query_ref.shape[0]
+    head_size = keys.shape[1]
+    span = keys.shape[0]
+    particles = amount // per_particle
+    lane = lax.broadcasted_iota(jnp.int32, side_ref.shape, 1)
+    side = jnp.zeros(side_ref.shape, jnp.float32)
+    for group in range(groups):
+        query = query_ref[:, group * head_size : (group + 1) * head_size]
+        scores = lax.dot_general(
+            query, keys, (((1,), (1,)), ((), ())), preferred_element_type=jnp.float32
+        ) * factor
+        scores = (scores.reshape(particles, per_particle, span) + bias[:, None, :]).reshape(
+            amount, span
         )
-    ).astype(jnp.bfloat16)
-
-
-def attend(query, keys, vals, lengths, tree_keys, tree_vals, tree_mask, factor, block=512):
-    amount, head_size = query.shape
-    span = keys.shape[0]
+        tree_scores = lax.dot_general(
+            query, tree_keys, (((1,), (1,)), ((), ())), preferred_element_type=jnp.float32
+        ) * factor
+        tree_scores = jnp.where(tree_visible, tree_scores, NEGATIVE)
+        high = jnp.maximum(
+            jnp.max(scores, axis=1, keepdims=True), jnp.max(tree_scores, axis=1, keepdims=True)
+        )
+        safe = jnp.where(high > 0.5 * NEGATIVE, high, 0.0)
+        weights = jnp.exp(scores - safe)
+        tree_weights = jnp.exp(tree_scores - safe)
+        total = jnp.sum(weights, axis=1, keepdims=True) + jnp.sum(
+            tree_weights, axis=1, keepdims=True
+        )
+        out_ref[:, group * head_size : (group + 1) * head_size] = (
+            jnp.dot(weights.astype(jnp.bfloat16), vals, preferred_element_type=jnp.float32)
+            + jnp.dot(
+                tree_weights.astype(jnp.bfloat16), tree_vals, preferred_element_type=jnp.float32
+            )
+        ).astype(jnp.bfloat16)
+        side = jnp.where(lane == group, total, side)
+        side = jnp.where(lane == groups + group, high, side)
+    out_ref[:, groups * head_size :] = jnp.zeros(
+        (amount, out_ref.shape[1] - groups * head_size), jnp.bfloat16
+    )
+    side_ref[...] = side
+
+
+def attend(queries, keys, vals, bias, tree_keys, tree_vals, tree_mask, factor, groups, per_particle,
+           block=256):
+    amount, width = queries.shape
+    span, head_size = keys.shape
     tree_amount = tree_keys.shape[0]
     whole = lambda i: (0, 0)
     rows = lambda i: (i, 0)
     return pl.pallas_call(
-        lambda *refs: attend_kernel(*refs, factor=factor),
+        lambda *refs: attend_kernel(*refs, factor=factor, groups=groups, per_particle=per_particle),
         out_shape=(
-            jax.ShapeDtypeStruct((amount, head_size), jnp.bfloat16),
-            jax.ShapeDtypeStruct((amount, 1), jnp.float32),
-            jax.ShapeDtypeStruct((amount, 1), jnp.float32),
+            jax.ShapeDtypeStruct((amount, width + 128), jnp.bfloat16),
+            jax.ShapeDtypeStruct((amount, 128), jnp.float32),
         ),
         grid=(amount // block,),
         in_specs=[
-            pl.BlockSpec((block, head_size), rows),
+            pl.BlockSpec((block, width), rows),
             pl.BlockSpec((span, head_size), whole),
             pl.BlockSpec((span, head_size), whole),
-            pl.BlockSpec((block, 1), rows),
+            pl.BlockSpec((block // per_particle, span), rows),
             pl.BlockSpec((tree_amount, head_size), whole),
             pl.BlockSpec((tree_amount, head_size), whole),
             pl.BlockSpec((block, tree_amount), rows),
         ],
         out_specs=(
-            pl.BlockSpec((block, head_size), rows),
-            pl.BlockSpec((block, 1), rows),
-            pl.BlockSpec((block, 1), rows),
+            pl.BlockSpec((block, width + 128), rows),
+            pl.BlockSpec((block, 128), rows),
         ),
         compiler_params=pltpu.CompilerParams(dimension_semantics=("arbitrary",)),
-    )(query, keys, vals, lengths, tree_keys, tree_vals, tree_mask)
+    )(queries, keys, vals, bias, tree_keys, tree_vals, tree_mask)
 
 
 def reduce_rows(value, axis):
@@ -156,24 +172,21 @@
     vals = context_values[:, 0, :]
     span = keys.shape[0]
     factor = 1.0 / math.sqrt(head_size)
-    lengths_rows = jnp.repeat(prefix_lengths, PROPOSALS)
-    lengths_query = jnp.repeat(lengths_rows - position * span, groups)[:, None]
-    tree_mask = jnp.repeat(
-        ancestry_columns(parents, position * row_share, row_share).astype(jnp.bfloat16), groups, axis=0
-    )
-    summed, high, weight_sum = attend(
-        queries.reshape(total_rows * groups, head_size), keys, vals, lengths_query,
-        tree_keys, tree_vals, tree_mask, factor,
-    )
-    high = high.reshape(total_rows, groups)
-    weight_sum = weight_sum.reshape(total_rows, groups)
+    positions = position * span + jnp.arange(span, dtype=jnp.int32)
+    bias = jnp.where(positions[None, :] < prefix_lengths[:, None], 0.0, NEGATIVE)
+    tree_mask = ancestry_columns(parents, position * row_share, row_share).astype(jnp.bfloat16)
+    packed_attn, side = attend(
+        queries, keys, vals, bias, tree_keys, tree_vals, tree_mask, factor, groups, PROPOSALS
+    )
+    weight_sum = side[:, :groups]
+    high = side[:, groups : 2 * groups]
     sum_hi = lax.reduce_precision(weight_sum, exponent_bits=8, mantissa_bits=7)
     sum_lo = weight_sum - sum_hi
     side_block = jnp.concatenate(
         [sum_hi, sum_lo, *split_three(high), jnp.zeros((total_rows, 128 - 5 * groups), jnp.float32)],
         axis=1,
     ).astype(jnp.bfloat16)
-    packed_attn = jnp.concatenate([summed.reshape(total_rows, query_width), side_block], axis=1)
+    packed_attn = lax.dynamic_update_slice(packed_attn, side_block, (0, query_width))
     count = lax.axis_size("ctx")
     moved = lax.all_to_all(packed_attn, "ctx", 0, 0, tiled=True).reshape(count, row_share, -1)
     moved = moved.astype(jnp.float32)

time: 203 us -> 179 us (0.88)
  Pallas kernels: 32.4 us -> 17.7 us
  local copies, waits for them, and re-layouts: 16.2 us -> 7.31 us
  other arithmetic: 16.2 us -> 13 us
    pallas_call x1, Pallas kernels: 32.4 us -> 17.7 us  [attend(): pl.pallas_call(lambda *refs: attend_kernel(*refs, factor=factor, groups=g...]
    pallas_call x2 -> x0, other arithmetic: 4.4 us -> none  [attend(): pl.pallas_call(lambda *refs: attend_kernel(*refs, factor=factor), out_sha...]
    all_to_all x1, waiting for transfers between devices: 35.5 us -> 39.4 us  [reduce_rows(): moved = lax.all_to_all(value, axis, 0, 0, tiled=True)]
    concatenate x2 -> x1, local copies, waits for them, and re-layouts: 4.07 us -> 0.31 us  [body(): jnp.concatenate([sum_hi, sum_lo, *split_three(high), jnp.zeros((total_row...]
    another operation x4 -> x0, local copies, waits for them, and re-layouts: 2.97 us -> none  [the longest x1 1.95 us: body(): lengths_query = jnp.repeat(lengths_rows - position * span, groups)[:, None]]
    reshape x5 -> x0, local copies, waits for them, and re-layouts: 2.84 us -> none  [the longest x1 1.28 us: body(): queries.reshape(total_rows * groups, head_size)]
where the time goes in v5:
time: 179 us; the launch traced here: 178 us
  blocking collectives  61.9 us (35%)
  waiting for transfers between devices  56.1 us (31%)
  Pallas kernels  17.7 us (10%)
  starting transfers between devices  16.4 us (9%)
  other arithmetic  13 us (7%)
  local copies, waits for them, and re-layouts  7.31 us (4%)
  matrix products  5.89 us (3%)
    all_to_all x1, waiting for transfers between devices, reduce_rows(): moved = lax.all_to_all(value, axis, 0, 0, tiled=True)  39.4 us
    all_to_all x1, blocking collectives, reduce_rows(): moved = lax.all_to_all(value, axis, 0, 0, tiled=True)  23 us
    all_to_all x1, blocking collectives, body(): lax.all_to_all(packed_attn, 'ctx', 0, 0, tiled=True)  21.7 us
    pallas_call x1, Pallas kernels, attend(): pl.pallas_call(lambda *refs: attend_kernel(*refs, factor=factor, groups=g...  17.7 us
    all_to_all x1, blocking collectives, gather_rows(): return lax.all_to_all(jnp.tile(value, (count, 1)), axis, 0, 0, tiled=True)  17.3 us
    all_to_all x1, waiting for transfers between devices, gather_rows(): return lax.all_to_all(jnp.tile(value, (count, 1)), axis, 0, 0, tiled=True)  11.5 us
    all_to_all x1, starting transfers between devices, reduce_rows(): moved = lax.all_to_all(value, axis, 0, 0, tiled=True)  8.28 us
    ppermute x1, waiting for transfers between devices, body(): other_rows = lax.ppermute(proposal_rows, 'sec', [(0, 1), (1, 0)])  5.14 us
  transfers between devices with their start and end apart: 3, of which 3 were waited for; matrix products, arithmetic and copies ran while one was open for 3% of the time, Pallas kernels for 0%

profile of v5, /device:TPU:1, one launch (start us, length us, event | category | flops | bytes accessed | tf_op | source)
XLA Modules:
  0.0 178.4 jit_solution(18310826137137582566)
XLA Ops:
  0.0 0.0 copy-start
  0.0 3.6 %collective-permute-start = (bf16[256,512]{1,0:T(8,128)(2,1)}, bf16[256,512]{1,0:T(8,128)(2,1)S(1)}, u32[]{:S(2)}, u32[]{:S(2)}) collective-permute-start(bf16[256,512]{1,0:T(8,128)(2,1)} %param.10), channel_id=1, source_target_pairs={{0,64},{64,0},{1,65},{65,1},{2,66},{66,2},{3,67},{67,3},{4,68},{68... | collective-permute-start | bytes 786440 | tf_op jit(solution)/shard_map/ppermute | solution.py:141
  3.6 0.7 convert_element_type.34
  4.3 5.1 %collective-permute-done = bf16[256,512]{1,0:T(8,128)(2,1)S(1)} collective-permute-done((bf16[256,512]{1,0:T(8,128)(2,1)}, bf16[256,512]{1,0:T(8,128)(2,1)S(1)}, u32[]{:S(2)}, u32[]{:S(2)}) %collective-permute-start) | collective-permute-done | bytes 262176 | tf_op jit(solution)/shard_map/ppermute | solution.py:141
  9.4 1.3 fusion.9
  10.7 0.1 broadcast_select_fusion
  10.8 2.4 %fusion.1 = f32[512,1280]{1,0:T(8,128)S(1)} fusion(bf16[512,128]{1,0:T(8,128)(2,1)} %bitcast.69, bf16[512,128]{1,0:T(8,128)(2,1)} %bitcast.70, bf16[512,1024]{1,0:T(8,128)(2,1)} %param.12, f32[512]{0:T(512)S(1)} %convert_element_type.34, bf16[256,512]{1,0:T(8,128)(2,1)S(1)} %collective-permute-done, bf16[256,512]{1,0:T(8,128)(2,1)} %param.10, pred[]{:T(512)S(6)} %eq.40), kind=kOutput, calls=%fused_computation.5 | convolution fusion | flops 678166528 | bytes 4458497 | tf_op jit(solution)/shard_map/dot_general | solution.py:156
  13.2 1.8 %pad_maximum_fusion = f32[512,1408]{1,0:T(8,128)} fusion(f32[512,128]{1,0:T(8,128)S(1)} %broadcast_select_fusion, f32[512,1280]{1,0:T(8,128)S(1)} %fusion.1), kind=kLoop, calls=%fused_computation.2 | loop fusion | flops 720896 | bytes 5767168 | tf_op jit(solution)/shard_map/concatenate | solution.py:160
  15.0 0.0 copy-start.3
  15.0 8.3 %all-to-all-start = ((f32[16,32,1408]{2,1,0:T(8,128)}), f32[16,32,1408]{2,1,0:T(8,128)}, u32[]{:S(2)}, u32[]{:S(2)}) async-start(f32[16,32,1408]{2,1,0:T(8,128)} %bitcast.63), calls=%async_computation | async-start | bytes 5767168 | tf_op jit(solution)/shard_map/all_to_all | solution.py:120
  23.3 0.0 copy-done.3
  23.3 0.6 convolution_compare_fusion.2
  23.9 39.4 %all-to-all-done = f32[16,32,1408]{2,1,0:T(8,128)} async-done(((f32[16,32,1408]{2,1,0:T(8,128)}), f32[16,32,1408]{2,1,0:T(8,128)}, u32[]{:S(2)}, u32[]{:S(2)}) %all-to-all-start) | async-done | bytes 2883616 | tf_op jit(solution)/shard_map/all_to_all | solution.py:120
  63.3 2.0 %reduce_sum.46 = f32[32,1408]{1,0:T(8,128)S(1)} reduce(f32[16,32,1408]{2,1,0:T(8,128)} %all-to-all-done, f32[]{:T(128)} %constant.17.clone.1), dimensions={0}, to_apply=%region_1.2 | reduce | flops 675840 | bytes 3063812 | tf_op jit(solution)/shard_map/reduce_sum | solution.py:121
  65.3 0.1 fusion.31
  65.4 0.1 fusion.22
  65.5 1.1 tile.4
  66.7 4.5 %all-to-all-start.1 = ((bf16[16,32,1024]{2,1,0:T(8,128)(2,1)}), bf16[16,32,1024]{2,1,0:T(8,128)(2,1)S(1)}, u32[]{:S(2)}, u32[]{:S(2)}) async-start(bf16[16,32,1024]{2,1,0:T(8,128)(2,1)} %tile.4), calls=%async_computation.1 | async-start | bytes 2097152 | tf_op jit(solution)/shard_map/all_to_all | solution.py:126
  71.2 0.0 copy-start.2
  71.2 1.1 convolution_compare_fusion
  72.3 1.1 fusion.7.refs_6_
  73.4 0.0 copy-done.2
  73.4 0.8 compare_select_fusion.refs_3_
  74.2 0.6 fusion.37
  74.8 11.5 %all-to-all-done.1 = bf16[16,32,1024]{2,1,0:T(8,128)(2,1)S(1)} async-done(((bf16[16,32,1024]{2,1,0:T(8,128)(2,1)}), bf16[16,32,1024]{2,1,0:T(8,128)(2,1)S(1)}, u32[]{:S(2)}, u32[]{:S(2)}) %all-to-all-start.1) | async-done | bytes 1048608 | tf_op jit(solution)/shard_map/all_to_all | solution.py:126
  86.3 0.0 copy-start.1
  86.3 1.0 copy-done.1
  87.3 17.7 %shard_map.100 = (bf16[512,1152]{1,0:T(8,128)(2,1)}, f32[512,128]{1,0:T(8,128)}) custom-call(bf16[512,1024]{1,0:T(8,128)(2,1)} %bitcast.64, bf16[2048,128]{1,0:T(8,128)(2,1)} %bitcast.67, bf16[2048,128]{1,0:T(8,128)(2,1)} %bitcast.68, f32[32,2048]{1,0:T(8,128)} %compare_select_fusion.refs_3_, bf16[32,128]{1,0:T(8,128)(2,1)} %get-tuple-element.17.refs_4_, ...), custom_call_target="tpu_custom_call" | custom-call | tf_op jit(solution)/shard_map/pallas_call | solution.py:94
  105.0 1.2 fusion.20
  106.2 0.3 concatenate.20
  106.6 0.7 constant_dynamic-update-slice_fusion
  107.2 21.7 %all_to_all.38 = bf16[16,32,1152]{2,1,0:T(8,128)(2,1)S(1)} all-to-all(bf16[16,32,1152]{2,1,0:T(8,128)(2,1)} %bitcast.65), channel_id=1, replica_groups=mesh['sec'=2,'head'=4,'ctx'=16] {'ctx'}, dimensions={0} | all-to-all | bytes 2359296 | tf_op jit(solution)/shard_map/all_to_all | solution.py:191
  128.9 3.3 %copy.30 = bf16[16,32,1152]{1,2,0:T(8,128)(2,1)} copy(bf16[16,32,1152]{2,1,0:T(8,128)(2,1)S(1)} %all_to_all.38) | data formatting | bytes 2359296 | tf_op jit(solution)/shard_map/all_to_all | solution.py:191
  132.2 3.3 %convert_element_type.37 = f32[16,32,1152]{1,2,0:T(8,128)S(1)} convert(bf16[16,32,1152]{1,2,0:T(8,128)(2,1)} %copy.30) | non-fusion elementwise | flops 589824 | bytes 3538944 | tf_op jit(solution)/shard_map/convert_element_type | solution.py:192
  135.5 0.9 fusion
  136.4 0.1 fusion.15
  136.5 0.1 copy.34
  136.6 0.1 tile.5
  136.7 17.3 %all_to_all.39 = bf16[16,32,1024]{2,1,0:T(8,128)(2,1)S(1)} all-to-all(bf16[16,32,1024]{2,1,0:T(8,128)(2,1)S(1)} %tile.5), channel_id=1, replica_groups=mesh['sec'=2,'head'=4,'ctx'=16] {'ctx'}, dimensions={0} | all-to-all | bytes 2097152 | tf_op jit(solution)/shard_map/all_to_all | solution.py:126
  154.0 0.0 copy-done
  154.0 0.7 fusion.10
  154.7 23.0 %all_to_all.40 = f32[8,64,512]{2,1,0:T(8,128)S(1)} all-to-all(f32[8,64,512]{2,1,0:T(8,128)S(1)} %fusion.10), channel_id=1, replica_groups=mesh['sec'=2,'head'=4,'ctx'=16] {'sec','head'}, dimensions={0} | all-to-all | bytes 2097152 | tf_op jit(solution)/shard_map/all_to_all | solution.py:120
  177.7 0.7 reduce_sum.49
  (7 shorter events, 0.1 us)
Async XLA Ops:
  0.0 154.0 %copy-start = (bf16[1024,512]{1,0:T(8,128)(2,1)S(1)}, bf16[1024,512]{1,0:T(8,128)(2,1)}, u32[]{:S(2)}) copy-start(bf16[1024,512]{1,0:T(8,128)(2,1)} %param.15) | copy-start | bytes 3145732
  0.0 9.4 %collective-permute-start = (bf16[256,512]{1,0:T(8,128)(2,1)}, bf16[256,512]{1,0:T(8,128)(2,1)S(1)}, u32[]{:S(2)}, u32[]{:S(2)}) collective-permute-start(bf16[256,512]{1,0:T(8,128)(2,1)} %param.10), channel_id=1, source_target_pairs={{0,64},{64,0},{1,65},{65,1},{2,66},{66,2},{3,67},{67,3},{4,68},{68... | collective-permute-start | bytes 786440 | tf_op jit(solution)/shard_map/ppermute | solution.py:141
  15.0 8.3 %copy-start.3 = (s32[512]{0:T(512)S(1)}, s32[512]{0:T(512)}, u32[]{:S(2)}) copy-start(s32[512]{0:T(512)} %param.19) | copy-start | bytes 6148
  15.0 48.4 %all-to-all-start = ((f32[16,32,1408]{2,1,0:T(8,128)}), f32[16,32,1408]{2,1,0:T(8,128)}, u32[]{:S(2)}, u32[]{:S(2)}) async-start(f32[16,32,1408]{2,1,0:T(8,128)} %bitcast.63), calls=%async_computation | async-start | bytes 5767168 | tf_op jit(solution)/shard_map/all_to_all | solution.py:120
  66.7 19.6 %all-to-all-start.1 = ((bf16[16,32,1024]{2,1,0:T(8,128)(2,1)}), bf16[16,32,1024]{2,1,0:T(8,128)(2,1)S(1)}, u32[]{:S(2)}, u32[]{:S(2)}) async-start(bf16[16,32,1024]{2,1,0:T(8,128)(2,1)} %tile.4), calls=%async_computation.1 | async-start | bytes 2097152 | tf_op jit(solution)/shard_map/all_to_all | solution.py:126
  71.2 2.2 %copy-start.2 = (s32[32]{0:T(128)S(1)}, s32[32]{0:T(128)}, u32[]{:S(2)}) copy-start(s32[32]{0:T(128)} %param.18) | copy-start | bytes 388
  86.3 1.0 copy-start.1
